TPU v7x, 32 devices: a whole 2x2x4 slice. The times are simulated.
32 devices in a mesh: patch: 8 (over z, y), band: 4 (over x, core).
Axes of the slice: x: 2, y: 2, z: 4, core: 2. Of those that a mesh axis runs over, the one named last changes fastest.
Arguments:
- exposures: float32 [64, 256, 128], P(('band', 'patch')), parts along dimension 0, may hold values from -6 to 6
- variance: float32 [64, 256, 128], P(('band', 'patch')), parts along dimension 0, may hold values from 0.01 to 60, as said below
- mask_bits: int32 [64, 256, 128], P(('band', 'patch')), parts along dimension 0, may hold values from 0 to 4095
- kernel_coeffs: float32 [64, 27, 6], P(('band', 'patch')), parts along dimension 0, may hold values from -3 to 3
- ccd_visit: int32 [64, 1], P(('band', 'patch')), parts along dimension 0, may hold values from 0 to 7
- strip_patch: int32 [2048, 1], P(('band', 'patch')), parts along dimension 0, may hold values from 0 to 7, as said below
- strip_row: int32 [2048], P(('band', 'patch')), parts along dimension 0, may hold values from 0 to 120
- strip_col: int32 [2048], P(('band', 'patch')), parts along dimension 0, may hold values from 0 to 384
Outputs:
- coadd_image: float32 [32, 128, 512], P(('band', 'patch')), parts along dimension 0
- weight_map: float32 [32, 128, 512], P(('band', 'patch')), parts along dimension 0
There are 4 independent parts, one for each index of `band`. A program takes and returns all parts, laid end to end along the dimension named above; each array names one. Nothing has to cross between parts.
Inputs may be any that keep to these rules, and one draw needn't show every extreme that they name: `variance`: Positive. `ccd_visit`: every visit has at least one CCD. `strip_patch`: among the strips of one device (aligned blocks of 64 rows) no patch is named more than 16 times; one patch is named exactly 16 times in every block.
All inputs are finite; a program needn't handle non-finite values.
Results may differ from a plain program's by a relative error of at most 0.00011.
Values sent between devices are 32-bit elements; how exact they have to be, the bound alone decides.
No kernel may reach another device: no remote copies, remote signals or barrier semaphores. Data moves between devices by JAX's collectives and lax.ppermute only.
A program may use at most 64 MiB of HBM per device.

v0:
```python
import math

import jax
import jax.numpy as jnp
from jax import lax
from jax.sharding import PartitionSpec as P

PH = 128
PW = 512
KS = 21
VISITS = 8


gauss_widths = (0.75, 1.5, 3.0)
largest_value = lax.Precision.HIGHEST


def tap_values(offsets, kernel_half_width):
    support = jnp.arange(-kernel_half_width, kernel_half_width + 1).astype(jnp.float32)
    inside = (jnp.abs(offsets) <= kernel_half_width).astype(jnp.float32)
    tables = []
    for spread in gauss_widths:
        gauss_total = jnp.sum(jnp.exp(-support * support / (2.0 * spread * spread)))
        profile = jnp.exp(-offsets * offsets / (2.0 * spread * spread)) / gauss_total * inside
        scaled = offsets / spread
        tables.append(jnp.stack([profile, profile * scaled, profile * scaled * scaled]))
    return jnp.stack(tables)


def row_filters(row_count, kernel_half_width):
    row_ids = jnp.arange(row_count)[:, None]
    window_ids = jnp.arange(row_count + 2 * kernel_half_width)[None, :]
    return tap_values(
        (window_ids - row_ids - kernel_half_width).astype(jnp.float32), kernel_half_width
    )


def column_filters(column_count, kernel_half_width):
    source = jnp.arange(column_count)[:, None]
    target_patch = jnp.arange(column_count)[None, :]
    return tap_values((source - target_patch).astype(jnp.float32), kernel_half_width)


def convolve(windows, kernel_terms, height):
    kernel_half_width = KS // 2
    batch_size = windows.shape[0]
    row_count = windows.shape[1] - 2 * kernel_half_width
    columns = windows.shape[2]
    smooth = jnp.einsum(
        "gaij,njc->ngaic",
        row_filters(row_count, kernel_half_width),
        windows,
        precision=largest_value,
    )
    column_ops = column_filters(columns, kernel_half_width)
    row_coords = jnp.arange(row_count).astype(jnp.float32)[None, :]
    y_plane = jnp.broadcast_to(
        (2.0 * row_coords / (height - 1) - 1.0)[:, :, None], (batch_size, row_count, columns)
    )
    x_line = 2.0 * jnp.arange(columns).astype(jnp.float32) / (columns - 1) - 1.0
    x_plane = jnp.broadcast_to(x_line[None, None, :], (batch_size, row_count, columns))
    ones_plane = jnp.ones((batch_size, row_count, columns), jnp.float32)
    poly_planes = jnp.stack(
        [ones_plane, x_plane, y_plane, x_plane * x_plane, x_plane * y_plane, y_plane * y_plane],
        axis=1,
    )
    kernel_split = kernel_terms.reshape(batch_size, 3, 9, kernel_terms.shape[2])
    result = jnp.zeros((batch_size, row_count, columns), jnp.float32)
    for gauss_index in range(3):
        basis_images = jnp.einsum(
            "naic,bcd->nabid",
            smooth[:, gauss_index],
            column_ops[gauss_index],
            precision=largest_value,
        )
        fields = jnp.einsum(
            "nkp,npid->nkid", kernel_split[:, gauss_index], poly_planes, precision=largest_value
        )
        fields = fields.reshape(batch_size, 3, 3, row_count, columns)
        result = result + jnp.sum(basis_images * fields, axis=(1, 2))
    return result


def place_slots(flux_flat, weight_flat, offsets, patch_rows, patch_cols):
    slot_total, strip_rows, columns = flux_flat.shape
    group = math.gcd(slot_total, 16)
    pairs = jnp.stack([flux_flat, weight_flat], axis=1).reshape(
        slot_total // group, group, 2, strip_rows, columns
    )
    grouped_offsets = offsets.reshape(slot_total // group, group, offsets.shape[1])
    target_cols = jnp.arange(patch_cols)
    source_cols = jnp.arange(columns)
    target_rows = jnp.arange(patch_rows)
    source_rows = jnp.arange(strip_rows)

    def place_group(total, item):
        pixel_block_tile, block_offsets = item
        column_selection = (
            target_cols[None, None, :]
            == block_offsets[:, 1][:, None, None] + source_cols[None, :, None]
        ).astype(jnp.float32)
        row_select = (
            target_rows[None, :, None]
            == block_offsets[:, 0][:, None, None] + source_rows[None, None, :]
        ).astype(jnp.float32)
        broadened_width = jnp.einsum(
            "vmwn,vny->vmwy", pixel_block_tile, column_selection, precision=largest_value
        )
        return (
            total
            + jnp.einsum("gri,gkip->krp", row_select, broadened_width, precision=largest_value),
            None,
        )

    start = jnp.zeros((2, patch_rows, patch_cols), jnp.float32)
    placed, _ = lax.scan(place_group, start, (pairs, grouped_offsets))
    return (placed[0], placed[1])


def shards(
    exposures, variance, mask_bits, kernel_coeffs, ccd_visit, strip_patch, strip_row, strip_col
):
    ccd_count, height, columns = exposures.shape
    strip_total = strip_patch.shape[0]
    per_ccd = strip_total // ccd_count
    strip_rows = height // per_ccd
    devices = lax.axis_size("patch")
    capacity = 2 * strip_total // devices
    kernel_half_width = KS // 2
    usable = (jnp.bitwise_and(mask_bits, 3) != 3).astype(jnp.float32)
    visit_hot = (ccd_visit == jnp.arange(VISITS)[None, :]).astype(jnp.float32)
    local_count = jnp.sum(jnp.sum(usable, axis=(1, 2))[:, None] * visit_hot, axis=0)
    local_load = jnp.sum(jnp.sum(usable * variance, axis=(1, 2))[:, None] * visit_hot, axis=0)
    visit_count, visit_load = lax.psum((local_count, local_load), "patch")
    visit_weight = (visit_count + 1.0) / (visit_load + 1.0)
    destination = strip_patch[:, 0]
    strip_ids = jnp.arange(strip_total)
    earlier = strip_ids[None, :] < strip_ids[:, None]
    same_target = destination[None, :] == destination[:, None]
    slot_rank = jnp.sum(jnp.logical_and(earlier, same_target).astype(jnp.int32), axis=1)
    slot_index = destination * capacity + slot_rank
    strip_visit = jnp.repeat(ccd_visit[:, 0], per_ccd)
    placement = jnp.stack([strip_row, strip_col, strip_visit], axis=1)

    def pack(values):
        holder = jnp.zeros((devices * capacity,) + values.shape[1:], values.dtype)
        return holder.at[slot_index].set(values).reshape((devices, capacity) + values.shape[1:])

    padded = jnp.pad(exposures, ((0, 0), (kernel_half_width, kernel_half_width), (0, 0)))
    weight_strips = usable.reshape(strip_total, strip_rows, columns)

    def match_ccd(ccd_pair):
        return convolve(ccd_pair[0][None], ccd_pair[1][None], height)[0]

    convolved = lax.map(match_ccd, (padded, kernel_coeffs))
    flux_strips = (usable * convolved).reshape(strip_total, strip_rows, columns)
    flux_slots, weight_slots, slot_meta = (
        lax.all_to_all(pack(flux_strips), "patch", split_axis=0, concat_axis=0, tiled=True),
        lax.all_to_all(pack(weight_strips), "patch", split_axis=0, concat_axis=0, tiled=True),
        lax.all_to_all(pack(placement), "patch", split_axis=0, concat_axis=0, tiled=True),
    )
    slot_total = flux_slots.shape[0] * flux_slots.shape[1]
    flux_flat = flux_slots.reshape(slot_total, strip_rows, columns)
    weight_flat = weight_slots.reshape(slot_total, strip_rows, columns)
    meta_flat = slot_meta.reshape(slot_total, 3)
    slot_hot = (meta_flat[:, 2:3] == jnp.arange(VISITS)[None, :]).astype(jnp.float32)
    slot_weight = jnp.sum(slot_hot * visit_weight[None, :], axis=1)
    flux_flat = slot_weight[:, None, None] * flux_flat
    weight_flat = slot_weight[:, None, None] * weight_flat
    numerator, weight_map = place_slots(flux_flat, weight_flat, meta_flat, PH, PW)
    coadd_image = numerator / jnp.maximum(weight_map, 1.0)
    return (coadd_image[None], weight_map[None])


def solution(mesh):
    return jax.shard_map(
        shards,
        mesh=mesh,
        in_specs=(
            P(("band", "patch"), None, None),
            P(("band", "patch"), None, None),
            P(("band", "patch"), None, None),
            P(("band", "patch"), None, None),
            P(("band", "patch"), None),
            P(("band", "patch"), None),
            P(("band", "patch")),
            P(("band", "patch")),
        ),
        out_specs=(P(("band", "patch"), None, None), P(("band", "patch"), None, None)),
        check_vma=False,
    )
```

profile of v0, /device:TPU:0, one launch (start us, length us, event | category | flops | bytes accessed | tf_op | source)
XLA Modules:
  0.0 163.5 jit_solution(13020536047330855543)
XLA Ops:
  0.6 0.9 convert_reduce_fusion.1
  2.2 0.7 broadcast_in_dim.57
  3.8 0.8 scatter_custom_fusion
  4.6 0.7 copy.83
  5.3 7.3 %all-to-all-start = ((s32[8,16,3]{1,2,0:T(4,128)}), s32[8,16,3]{1,2,0:T(4,128)S(1)}, u32[]{:S(2)}, u32[]{:S(2)}) async-start(s32[8,16,3]{1,2,0:T(4,128)} %copy.83), calls=%async_computation | async-start | bytes 32768 | tf_op jit(solution)/shard_map/all_to_all | solution.py:160
  12.6 1.0 pad.4
  13.6 74.2 %while.28 = (s32[]{:T(128)}, f32[2,256,128]{2,1,0:T(8,128)}, f32[2,276,128]{2,1,0:T(8,128)S(1)}, f32[2,27,6]{1,0,2:T(2,128)}) while((s32[]{:T(128)}, f32[2,256,128]{2,1,0:T(8,128)}, f32[2,276,128]{2,1,0:T(8,128)S(1)}, f32[2,27,6]{1,0,2:T(2,128)}) %tuple.104), condition=%wide.region_16.17_spmd.clone, body=%wide.region_9.16_spmd.sunk.clone | while | flops 2410444800 | bytes 36327148 | solution.py:155
  14.2 0.8 divide_select_fusion.18
  15.0 0.8 fusion.152
  16.5 0.8 divide_select_fusion.19
  17.4 0.8 fusion.153
  20.4 3.2 %fusion.155 = f32[1,3,3,256,128]{3,4,2,1,0:T(8,128)} fusion(f32[1,3,256,276]{2,3,1,0:T(8,128)S(1)} %maximum_bitcast_fusion.24, f32[1,3,256,276]{2,3,1,0:T(8,128)S(1)} %maximum_bitcast_fusion.25, f32[1,3,256,276]{2,3,1,0:T(8,128)S(1)} %maximum_bitcast_fusion.26, f32[2,276,128]{2,1,0:T(8,128)S(1)} %get-tuple-element.376, s32[]{:T(128)} %get-tuple-element.370), kind=kOutput, calls=%fused_computation.29.clone.1.clone | convolution fusion | flops 978020352 | bytes 3903492 | tf_op jit(solution)/shard_map/while/body/eval_jaxpr/gaij,njc->ngaic/dot_general | solution.py:49
  24.9 1.2 stack.128
  26.4 2.4 %fusion.158 = f32[3,3,256,128]{3,1,2,0:T(4,128)S(1)} fusion(f32[1,6,256,128]{3,1,2,0:T(8,128)S(1)} %stack.128, f32[3,3,6,1]{2,1,0,3:T(4,128)S(1)} %reshape.729), kind=kOutput, calls=%fused_computation.43.clone.1.clone | convolution fusion | flops 21233664 | bytes 1966296 | tf_op jit(solution)/shard_map/while/body/eval_jaxpr/nkp,npid->nkid/dot_general | solution.py:76
  28.8 1.5 copy.132
  31.5 2.5 %fusion.160 = f32[256,128]{0,1:T(8,128)S(1)} fusion(f32[3,3,256,128]{2,3,0,1:T(8,128)} %copy.132, f32[1,3,3,256,128]{3,4,2,1,0:T(8,128)} %fusion.155, f32[1,128,128]{1,2,0:T(8,128)S(1)} %get-tuple-element.342, f32[1,128,128]{1,2,0:T(8,128)S(1)} %fusion.159, f32[1,128,128]{1,2,0:T(8,128)S(1)} %get-tuple-element.343), kind=kOutput, calls=%fused_computation.38.clone.1.clone | convolution fusion | flops 453640192 | bytes 1900544 | tf_op jit(solution)/shard_map/while/body/eval_jaxpr/naic,bcd->nabid/dot_general | solution.py:70
  34.1 2.4 %fusion.161 = f32[3,3,256,128]{3,1,2,0:T(4,128)S(1)} fusion(f32[1,6,256,128]{3,1,2,0:T(8,128)S(1)} %stack.128, f32[3,3,6,1]{2,1,0,3:T(4,128)S(1)} %reshape.730), kind=kOutput, calls=%fused_computation.41.clone.1.clone | convolution fusion | flops 21233664 | bytes 1966296 | tf_op jit(solution)/shard_map/while/body/eval_jaxpr/nkp,npid->nkid/dot_general | solution.py:76
  36.5 1.5 copy.134
  38.0 0.7 divide_select_fusion.23
  38.7 0.7 fusion.162
  39.4 2.5 %fusion.163 = f32[256,128]{0,1:T(8,128)S(1)} fusion(f32[3,3,256,128]{2,3,0,1:T(8,128)} %copy.134, f32[1,3,3,256,128]{3,4,2,1,0:T(8,128)} %fusion.155, f32[1,128,128]{1,2,0:T(8,128)S(1)} %get-tuple-element.345, f32[1,128,128]{1,2,0:T(8,128)S(1)} %fusion.162, f32[1,128,128]{1,2,0:T(8,128)S(1)} %get-tuple-element.346), kind=kOutput, calls=%fused_computation.37.clone.1.clone | convolution fusion | flops 453640192 | bytes 1900544 | tf_op jit(solution)/shard_map/while/body/eval_jaxpr/naic,bcd->nabid/dot_general | solution.py:70
  42.0 2.4 %fusion.151 = f32[3,3,256,128]{3,1,2,0:T(4,128)S(1)} fusion(f32[1,6,256,128]{3,1,2,0:T(8,128)S(1)} %stack.128, f32[3,3,6,1]{2,1,0,3:T(4,128)S(1)} %reshape.728), kind=kOutput, calls=%fused_computation.39.clone.1.clone | convolution fusion | flops 21233664 | bytes 1966296 | tf_op jit(solution)/shard_map/while/body/eval_jaxpr/nkp,npid->nkid/dot_general | solution.py:76
  44.5 1.5 copy.130
  47.3 2.5 %fusion.157 = f32[256,128]{0,1:T(8,128)S(1)} fusion(f32[3,3,256,128]{2,3,0,1:T(8,128)} %copy.130, f32[1,3,3,256,128]{3,4,2,1,0:T(8,128)} %fusion.155, f32[1,128,128]{1,2,0:T(8,128)S(1)} %get-tuple-element.339, f32[1,128,128]{1,2,0:T(8,128)S(1)} %fusion.156, f32[1,128,128]{1,2,0:T(8,128)S(1)} %get-tuple-element.340), kind=kOutput, calls=%fused_computation.36.clone.1.clone | convolution fusion | flops 453640192 | bytes 1900544 | tf_op jit(solution)/shard_map/while/body/eval_jaxpr/naic,bcd->nabid/dot_general | solution.py:70
  51.3 0.8 divide_select_fusion.18
  52.1 0.8 fusion.152
  53.6 0.8 divide_select_fusion.19
  54.5 0.8 fusion.153
  57.5 3.2 %fusion.155 = f32[1,3,3,256,128]{3,4,2,1,0:T(8,128)} fusion(f32[1,3,256,276]{2,3,1,0:T(8,128)S(1)} %maximum_bitcast_fusion.24, f32[1,3,256,276]{2,3,1,0:T(8,128)S(1)} %maximum_bitcast_fusion.25, f32[1,3,256,276]{2,3,1,0:T(8,128)S(1)} %maximum_bitcast_fusion.26, f32[2,276,128]{2,1,0:T(8,128)S(1)} %get-tuple-element.376, s32[]{:T(128)} %get-tuple-element.370), kind=kOutput, calls=%fused_computation.29.clone.1.clone | convolution fusion | flops 978020352 | bytes 3903492 | tf_op jit(solution)/shard_map/while/body/eval_jaxpr/gaij,njc->ngaic/dot_general | solution.py:49
  62.0 1.2 stack.128
  63.5 2.4 %fusion.158 = f32[3,3,256,128]{3,1,2,0:T(4,128)S(1)} fusion(f32[1,6,256,128]{3,1,2,0:T(8,128)S(1)} %stack.128, f32[3,3,6,1]{2,1,0,3:T(4,128)S(1)} %reshape.729), kind=kOutput, calls=%fused_computation.43.clone.1.clone | convolution fusion | flops 21233664 | bytes 1966296 | tf_op jit(solution)/shard_map/while/body/eval_jaxpr/nkp,npid->nkid/dot_general | solution.py:76
  65.9 1.5 copy.132
  68.5 2.5 %fusion.160 = f32[256,128]{0,1:T(8,128)S(1)} fusion(f32[3,3,256,128]{2,3,0,1:T(8,128)} %copy.132, f32[1,3,3,256,128]{3,4,2,1,0:T(8,128)} %fusion.155, f32[1,128,128]{1,2,0:T(8,128)S(1)} %get-tuple-element.342, f32[1,128,128]{1,2,0:T(8,128)S(1)} %fusion.159, f32[1,128,128]{1,2,0:T(8,128)S(1)} %get-tuple-element.343), kind=kOutput, calls=%fused_computation.38.clone.1.clone | convolution fusion | flops 453640192 | bytes 1900544 | tf_op jit(solution)/shard_map/while/body/eval_jaxpr/naic,bcd->nabid/dot_general | solution.py:70
  71.2 2.4 %fusion.161 = f32[3,3,256,128]{3,1,2,0:T(4,128)S(1)} fusion(f32[1,6,256,128]{3,1,2,0:T(8,128)S(1)} %stack.128, f32[3,3,6,1]{2,1,0,3:T(4,128)S(1)} %reshape.730), kind=kOutput, calls=%fused_computation.41.clone.1.clone | convolution fusion | flops 21233664 | bytes 1966296 | tf_op jit(solution)/shard_map/while/body/eval_jaxpr/nkp,npid->nkid/dot_general | solution.py:76
  73.6 1.5 copy.134
  75.0 0.7 divide_select_fusion.23
  75.8 0.7 fusion.162
  76.5 2.5 %fusion.163 = f32[256,128]{0,1:T(8,128)S(1)} fusion(f32[3,3,256,128]{2,3,0,1:T(8,128)} %copy.134, f32[1,3,3,256,128]{3,4,2,1,0:T(8,128)} %fusion.155, f32[1,128,128]{1,2,0:T(8,128)S(1)} %get-tuple-element.345, f32[1,128,128]{1,2,0:T(8,128)S(1)} %fusion.162, f32[1,128,128]{1,2,0:T(8,128)S(1)} %get-tuple-element.346), kind=kOutput, calls=%fused_computation.37.clone.1.clone | convolution fusion | flops 453640192 | bytes 1900544 | tf_op jit(solution)/shard_map/while/body/eval_jaxpr/naic,bcd->nabid/dot_general | solution.py:70
  79.1 2.4 %fusion.151 = f32[3,3,256,128]{3,1,2,0:T(4,128)S(1)} fusion(f32[1,6,256,128]{3,1,2,0:T(8,128)S(1)} %stack.128, f32[3,3,6,1]{2,1,0,3:T(4,128)S(1)} %reshape.728), kind=kOutput, calls=%fused_computation.39.clone.1.clone | convolution fusion | flops 21233664 | bytes 1966296 | tf_op jit(solution)/shard_map/while/body/eval_jaxpr/nkp,npid->nkid/dot_general | solution.py:76
  81.6 1.5 copy.130
  84.4 2.5 %fusion.157 = f32[256,128]{0,1:T(8,128)S(1)} fusion(f32[3,3,256,128]{2,3,0,1:T(8,128)} %copy.130, f32[1,3,3,256,128]{3,4,2,1,0:T(8,128)} %fusion.155, f32[1,128,128]{1,2,0:T(8,128)S(1)} %get-tuple-element.339, f32[1,128,128]{1,2,0:T(8,128)S(1)} %fusion.156, f32[1,128,128]{1,2,0:T(8,128)S(1)} %get-tuple-element.340), kind=kOutput, calls=%fused_computation.36.clone.1.clone | convolution fusion | flops 453640192 | bytes 1900544 | tf_op jit(solution)/shard_map/while/body/eval_jaxpr/naic,bcd->nabid/dot_general | solution.py:70
  87.8 1.0 broadcast_select_fusion
  88.8 0.8 broadcast.1262.clone.1
  89.7 6.4 %scatter_fusion.1 = f32[128,8,128]{2,1,0:T(8,128)} fusion(f32[128,8,128]{2,1,0:T(8,128)} %broadcast.1262.clone.1, s32[64]{0:T(128)S(1)} %fusion.77, f32[64,8,128]{2,1,0:T(8,128)S(1)} %bitcast.242), kind=kCustom, calls=%fused_computation.2 | custom fusion | bytes 786688 | tf_op jit(solution)/shard_map/scatter | solution.py:147
  96.1 6.1 %all-to-all-start.2 = ((f32[8,16,8,128]{3,2,1,0:T(8,128)}), f32[8,16,8,128]{3,2,1,0:T(8,128)S(1)}, u32[]{:S(2)}, u32[]{:S(2)}) async-start(f32[8,16,8,128]{3,2,1,0:T(8,128)} %bitcast.49), calls=%async_computation.2 | async-start | bytes 1048576 | tf_op jit(solution)/shard_map/all_to_all | solution.py:159
  102.1 0.8 broadcast.1262.clone
  103.0 6.4 %scatter_fusion = f32[128,8,128]{2,1,0:T(8,128)} fusion(f32[128,8,128]{2,1,0:T(8,128)} %broadcast.1262.clone, s32[64]{0:T(128)S(1)} %fusion.77, f32[64,8,128]{2,1,0:T(8,128)S(1)} %bitcast.243), kind=kCustom, calls=%fused_computation.1 | custom fusion | bytes 786688 | tf_op jit(solution)/shard_map/scatter | solution.py:147
  109.4 6.6 %all-to-all-done.2 = f32[8,16,8,128]{3,2,1,0:T(8,128)S(1)} async-done(((f32[8,16,8,128]{3,2,1,0:T(8,128)}), f32[8,16,8,128]{3,2,1,0:T(8,128)S(1)}, u32[]{:S(2)}, u32[]{:S(2)}) %all-to-all-start.2) | async-done | bytes 524320 | tf_op jit(solution)/shard_map/all_to_all | solution.py:159
  116.0 3.6 %all-to-all-start.1 = ((f32[8,16,8,128]{3,2,1,0:T(8,128)}), f32[8,16,8,128]{3,2,1,0:T(8,128)S(1)}, u32[]{:S(2)}, u32[]{:S(2)}) async-start(f32[8,16,8,128]{3,2,1,0:T(8,128)} %bitcast.45), calls=%async_computation.1 | async-start | bytes 1048576 | tf_op jit(solution)/shard_map/all_to_all | solution.py:158
  119.9 22.9 %all-reduce.1 = (f32[8]{0:T(128)S(1)}, f32[8]{0:T(128)S(1)}) all-reduce(f32[8]{0:T(128)S(1)} %get-tuple-element.201, f32[8]{0:T(128)S(1)} %get-tuple-element.200), channel_id=1, replica_groups=mesh['patch'=8,'band'=4] {'patch'}, use_global_device_ids=true, to_apply=%region_7.8 | all-reduce | flops 16 | bytes 128 | tf_op jit(solution)/shard_map/psum | solution.py:134
  143.5 19.0 %while.29 = (s32[]{:T(128)}, f32[2,128,512]{1,2,0:T(8,128)S(1)}, f32[8,16,2,8,128]{4,3,2,1,0:T(8,128)S(1)}, s32[8,16,3]{1,2,0:T(4,128)S(1)}) while((s32[]{:T(128)}, f32[2,128,512]{1,2,0:T(8,128)S(1)}, f32[8,16,2,8,128]{4,3,2,1,0:T(8,128)S(1)}, s32[8,16,3]{1,2,0:T(4,128)S(1)}) %tuple.107), condition=%wide.region_20.21_spmd.clone.clone.clone, body=%wide.region_19.20_spmd.clone.clone.sunk.clone | while | flops 403982464 | bytes 2246471 | solution.py:116
  143.6 1.5 fusion.168
  145.1 0.7 fusion.169
  146.0 1.5 fusion.168
  147.5 0.7 fusion.169
  148.3 1.5 fusion.168
  149.9 0.7 fusion.169
  150.7 1.5 fusion.168
  152.2 0.7 fusion.169
  153.1 1.5 fusion.168
  155.4 1.5 fusion.168
  157.8 1.5 fusion.168
  160.2 1.5 fusion.168
  162.7 0.8 slice_divide_fusion
  (142 shorter events, 23.8 us)
Async XLA Ops:
  5.3 90.8 %all-to-all-start = ((s32[8,16,3]{1,2,0:T(4,128)}), s32[8,16,3]{1,2,0:T(4,128)S(1)}, u32[]{:S(2)}, u32[]{:S(2)}) async-start(s32[8,16,3]{1,2,0:T(4,128)} %copy.83), calls=%async_computation | async-start | bytes 32768 | tf_op jit(solution)/shard_map/all_to_all | solution.py:160
  13.6 74.2 %copy-start.1 = (s32[2,256,128]{2,1,0:T(8,128)S(1)}, s32[2,256,128]{2,1,0:T(8,128)}, u32[]{:S(2)}) copy-start(s32[2,256,128]{2,1,0:T(8,128)} %param.14) | copy-start | bytes 786436
  24.3 1.9 %copy-start.4 = (f32[2,27,6]{1,0,2:T(2,128)S(1)}, f32[2,27,6]{1,0,2:T(2,128)}, u32[]{:S(2)}) copy-start(f32[2,27,6]{1,0,2:T(2,128)} %get-tuple-element.377) | copy-start | bytes 3892 | tf_op jit(solution)/shard_map/while
  47.3 2.7 %copy-start.2 = (f32[2,256,128]{2,1,0:T(8,128)S(1)}, f32[2,256,128]{2,1,0:T(8,128)}, u32[]{:S(2)}) copy-start(f32[2,256,128]{2,1,0:T(8,128)} %get-tuple-element.371) | copy-start | bytes 786436 | tf_op jit(solution)/shard_map/while
  50.0 0.7 copy-start.3
  61.4 1.9 %copy-start.4 = (f32[2,27,6]{1,0,2:T(2,128)S(1)}, f32[2,27,6]{1,0,2:T(2,128)}, u32[]{:S(2)}) copy-start(f32[2,27,6]{1,0,2:T(2,128)} %get-tuple-element.377) | copy-start | bytes 3892 | tf_op jit(solution)/shard_map/while
  84.3 2.7 %copy-start.2 = (f32[2,256,128]{2,1,0:T(8,128)S(1)}, f32[2,256,128]{2,1,0:T(8,128)}, u32[]{:S(2)}) copy-start(f32[2,256,128]{2,1,0:T(8,128)} %get-tuple-element.371) | copy-start | bytes 786436 | tf_op jit(solution)/shard_map/while
  87.1 0.7 copy-start.3
  96.1 20.0 %all-to-all-start.2 = ((f32[8,16,8,128]{3,2,1,0:T(8,128)}), f32[8,16,8,128]{3,2,1,0:T(8,128)S(1)}, u32[]{:S(2)}, u32[]{:S(2)}) async-start(f32[8,16,8,128]{3,2,1,0:T(8,128)} %bitcast.49), calls=%async_computation.2 | async-start | bytes 1048576 | tf_op jit(solution)/shard_map/all_to_all | solution.py:159
  102.1 17.6 %copy-start = (f32[2,256,128]{2,1,0:T(8,128)S(1)}, f32[2,256,128]{2,1,0:T(8,128)}, u32[]{:S(2)}) copy-start(f32[2,256,128]{2,1,0:T(8,128)} %param.13) | copy-start | bytes 786436
  103.0 16.9 %copy-start.5 = (s32[2,1]{0,1:T(1,128)S(1)}, s32[2,1]{0,1:T(1,128)}, u32[]{:S(2)}) copy-start(s32[2,1]{0,1:T(1,128)} %param.16) | copy-start | bytes 28
  116.0 27.1 %all-to-all-start.1 = ((f32[8,16,8,128]{3,2,1,0:T(8,128)}), f32[8,16,8,128]{3,2,1,0:T(8,128)S(1)}, u32[]{:S(2)}, u32[]{:S(2)}) async-start(f32[8,16,8,128]{3,2,1,0:T(8,128)} %bitcast.45), calls=%async_computation.1 | async-start | bytes 1048576 | tf_op jit(solution)/shard_map/all_to_all | solution.py:158
where the time goes:
time: 165 us; the launch traced here: 163 us
  matrix products  53.4 us (32%)
  local copies, waits for them, and re-layouts  33.8 us (20%)
  other arithmetic  28.1 us (17%)
  blocking collectives  22.9 us (14%)
  starting transfers between devices  17 us (10%)
  waiting for transfers between devices  6.63 us (4%)
    psum x1, blocking collectives, shards(): visit_count, visit_load = lax.psum((local_count, local_load), 'patch')  22.9 us
    dot_general x6, matrix products, convolve(): jnp.einsum('naic,bcd->nabid', smooth[:, gauss_index], column_ops[gauss_in...  15 us
    dot_general x6, matrix products, convolve(): jnp.einsum('nkp,npid->nkid', kernel_split[:, gauss_index], poly_planes, p...  14.6 us
    scatter x3, local copies, waits for them, and re-layouts, pack(): holder.at[slot_index].set(values)  13.6 us
    dot_general x8, matrix products, place_group(): jnp.einsum('vmwn,vny->vmwy', pixel_block_tile, column_selection, precisio...  11.7 us
    dot_general x6, local copies, waits for them, and re-layouts, convolve(): jnp.einsum('nkp,npid->nkid', kernel_split[:, gauss_index], poly_planes, p...  8.72 us
    mul x12, other arithmetic, tap_values(): jnp.exp(-offsets * offsets / (2.0 * spread * spread)) / gauss_total * inside  8.62 us
    mul x12, other arithmetic, tap_values(): profile * scaled  8.56 us
  transfers between devices with their start and end apart: 3, of which 1 were waited for; matrix products, arithmetic and copies ran while one was open for 55% of the time, Pallas kernels for 0%

commit v1 on v0

--- a/solution.py
+++ b/solution.py
@@ -13,6 +13,7 @@
 
 gauss_widths = (0.75, 1.5, 3.0)
 largest_value = lax.Precision.HIGHEST
+mxu_value = lax.Precision.HIGH
 
 
 def tap_values(offsets, kernel_half_width):
@@ -41,44 +42,34 @@
     return tap_values((source - target_patch).astype(jnp.float32), kernel_half_width)
 
 
-def convolve(windows, kernel_terms, height):
+def convolve_all(padded, kernel_coeffs, height):
     kernel_half_width = KS // 2
-    batch_size = windows.shape[0]
-    row_count = windows.shape[1] - 2 * kernel_half_width
-    columns = windows.shape[2]
-    smooth = jnp.einsum(
-        "gaij,njc->ngaic",
-        row_filters(row_count, kernel_half_width),
-        windows,
-        precision=largest_value,
+    n, _, columns = padded.shape
+    rows = row_filters(height, kernel_half_width).reshape(9, height, height + 2 * kernel_half_width)
+    smooth = jnp.einsum("krj,njx->nkrx", rows, padded, precision=mxu_value)
+    col_ops = column_filters(columns, kernel_half_width)
+    x_line = 2.0 * jnp.arange(columns).astype(jnp.float32) / (columns - 1) - 1.0
+    coef = kernel_coeffs.reshape(n, 3, 3, 3, 6)
+    c = [coef[..., p, None] for p in range(6)]
+    fx = jnp.stack(
+        [
+            c[0] + c[1] * x_line + c[3] * (x_line * x_line),
+            c[2] + c[4] * x_line,
+            jnp.broadcast_to(c[5], c[0].shape[:-1] + (columns,)),
+        ],
+        axis=4,
     )
-    column_ops = column_filters(columns, kernel_half_width)
-    row_coords = jnp.arange(row_count).astype(jnp.float32)[None, :]
-    y_plane = jnp.broadcast_to(
-        (2.0 * row_coords / (height - 1) - 1.0)[:, :, None], (batch_size, row_count, columns)
+    mixed = jnp.sum(
+        col_ops[None, :, None, :, :, None, :] * fx[:, :, :, :, None, :, :], axis=3
     )
-    x_line = 2.0 * jnp.arange(columns).astype(jnp.float32) / (columns - 1) - 1.0
-    x_plane = jnp.broadcast_to(x_line[None, None, :], (batch_size, row_count, columns))
-    ones_plane = jnp.ones((batch_size, row_count, columns), jnp.float32)
-    poly_planes = jnp.stack(
-        [ones_plane, x_plane, y_plane, x_plane * x_plane, x_plane * y_plane, y_plane * y_plane],
-        axis=1,
+    mixed = mixed.reshape(n, 9, columns, 3 * columns)
+    fields = jnp.einsum("nkry,nkyz->nrz", smooth, mixed, precision=mxu_value)
+    y_line = (2.0 * jnp.arange(height).astype(jnp.float32) / (height - 1) - 1.0)[None, :, None]
+    return (
+        fields[:, :, :columns]
+        + y_line * fields[:, :, columns : 2 * columns]
+        + (y_line * y_line) * fields[:, :, 2 * columns :]
     )
-    kernel_split = kernel_terms.reshape(batch_size, 3, 9, kernel_terms.shape[2])
-    result = jnp.zeros((batch_size, row_count, columns), jnp.float32)
-    for gauss_index in range(3):
-        basis_images = jnp.einsum(
-            "naic,bcd->nabid",
-            smooth[:, gauss_index],
-            column_ops[gauss_index],
-            precision=largest_value,
-        )
-        fields = jnp.einsum(
-            "nkp,npid->nkid", kernel_split[:, gauss_index], poly_planes, precision=largest_value
-        )
-        fields = fields.reshape(batch_size, 3, 3, row_count, columns)
-        result = result + jnp.sum(basis_images * fields, axis=(1, 2))
-    return result
 
 
 def place_slots(flux_flat, weight_flat, offsets, patch_rows, patch_cols):
@@ -131,43 +122,51 @@
     visit_hot = (ccd_visit == jnp.arange(VISITS)[None, :]).astype(jnp.float32)
     local_count = jnp.sum(jnp.sum(usable, axis=(1, 2))[:, None] * visit_hot, axis=0)
     local_load = jnp.sum(jnp.sum(usable * variance, axis=(1, 2))[:, None] * visit_hot, axis=0)
-    visit_count, visit_load = lax.psum((local_count, local_load), "patch")
-    visit_weight = (visit_count + 1.0) / (visit_load + 1.0)
+
     destination = strip_patch[:, 0]
     strip_ids = jnp.arange(strip_total)
     earlier = strip_ids[None, :] < strip_ids[:, None]
     same_target = destination[None, :] == destination[:, None]
     slot_rank = jnp.sum(jnp.logical_and(earlier, same_target).astype(jnp.int32), axis=1)
     slot_index = destination * capacity + slot_rank
-    strip_visit = jnp.repeat(ccd_visit[:, 0], per_ccd)
-    placement = jnp.stack([strip_row, strip_col, strip_visit], axis=1)
-
-    def pack(values):
-        holder = jnp.zeros((devices * capacity,) + values.shape[1:], values.dtype)
-        return holder.at[slot_index].set(values).reshape((devices, capacity) + values.shape[1:])
+    slot_total = devices * capacity
+    chooser = (slot_index[None, :] == jnp.arange(slot_total)[:, None]).astype(jnp.float32)
 
     padded = jnp.pad(exposures, ((0, 0), (kernel_half_width, kernel_half_width), (0, 0)))
-    weight_strips = usable.reshape(strip_total, strip_rows, columns)
-
-    def match_ccd(ccd_pair):
-        return convolve(ccd_pair[0][None], ccd_pair[1][None], height)[0]
-
-    convolved = lax.map(match_ccd, (padded, kernel_coeffs))
-    flux_strips = (usable * convolved).reshape(strip_total, strip_rows, columns)
-    flux_slots, weight_slots, slot_meta = (
-        lax.all_to_all(pack(flux_strips), "patch", split_axis=0, concat_axis=0, tiled=True),
-        lax.all_to_all(pack(weight_strips), "patch", split_axis=0, concat_axis=0, tiled=True),
-        lax.all_to_all(pack(placement), "patch", split_axis=0, concat_axis=0, tiled=True),
+    convolved = convolve_all(padded, kernel_coeffs, height)
+    tiles = jnp.concatenate(
+        [
+            (usable * convolved).reshape(strip_total, strip_rows, columns),
+            usable.reshape(strip_total, strip_rows, columns),
+        ],
+        axis=1,
+    ).reshape(strip_total, 2 * strip_rows * columns)
+    packed = jnp.dot(chooser, tiles, precision=largest_value).reshape(
+        devices, capacity * 2 * strip_rows, columns
     )
-    slot_total = flux_slots.shape[0] * flux_slots.shape[1]
-    flux_flat = flux_slots.reshape(slot_total, strip_rows, columns)
-    weight_flat = weight_slots.reshape(slot_total, strip_rows, columns)
-    meta_flat = slot_meta.reshape(slot_total, 3)
-    slot_hot = (meta_flat[:, 2:3] == jnp.arange(VISITS)[None, :]).astype(jnp.float32)
+    strip_visit = jnp.repeat(ccd_visit[:, 0], per_ccd)
+    placement = jnp.stack([strip_row, strip_col, strip_visit], axis=1).astype(jnp.float32)
+    slot_meta = jnp.dot(chooser, placement, precision=largest_value).reshape(devices, capacity, 3)
+    meta = jnp.zeros((devices, 8, columns), jnp.float32)
+    meta = meta.at[:, 0:3, :capacity].set(jnp.swapaxes(slot_meta, 1, 2))
+    meta = meta.at[:, 3, :VISITS].set(jnp.broadcast_to(local_count, (devices, VISITS)))
+    meta = meta.at[:, 4, :VISITS].set(jnp.broadcast_to(local_load, (devices, VISITS)))
+    payload = jnp.concatenate([packed, meta], axis=1)
+    got = lax.all_to_all(payload, "patch", split_axis=0, concat_axis=0, tiled=True)
+    body_rows = capacity * 2 * strip_rows
+    got_meta = got[:, body_rows:, :]
+    visit_count = jnp.sum(got_meta[:, 3, :VISITS], axis=0)
+    visit_load = jnp.sum(got_meta[:, 4, :VISITS], axis=0)
+    visit_weight = (visit_count + 1.0) / (visit_load + 1.0)
+    slot_rows = got_meta[:, 0, :capacity].reshape(slot_total).astype(jnp.int32)
+    slot_cols = got_meta[:, 1, :capacity].reshape(slot_total).astype(jnp.int32)
+    slot_visit = got_meta[:, 2, :capacity].reshape(slot_total).astype(jnp.int32)
+    slot_hot = (slot_visit[:, None] == jnp.arange(VISITS)[None, :]).astype(jnp.float32)
     slot_weight = jnp.sum(slot_hot * visit_weight[None, :], axis=1)
-    flux_flat = slot_weight[:, None, None] * flux_flat
-    weight_flat = slot_weight[:, None, None] * weight_flat
-    numerator, weight_map = place_slots(flux_flat, weight_flat, meta_flat, PH, PW)
+    body = got[:, :body_rows, :].reshape(slot_total, 2, strip_rows, columns)
+    body = body * slot_weight[:, None, None, None]
+    offsets = jnp.stack([slot_rows, slot_cols], axis=1)
+    numerator, weight_map = place_slots(body[:, 0], body[:, 1], offsets, PH, PW)
     coadd_image = numerator / jnp.maximum(weight_map, 1.0)
     return (coadd_image[None], weight_map[None])
 

time: 165 us -> 93.3 us (0.57)
  matrix products: 53.4 us -> 24.6 us
  local copies, waits for them, and re-layouts: 33.8 us -> 7.52 us
  blocking collectives: 22.9 us -> 0 us
  waiting for transfers between devices: 6.63 us -> 26.5 us
  starting transfers between devices: 17 us -> 7.31 us
  other arithmetic: 28.1 us -> 25.6 us
    dot_general x14 -> x4, matrix products: 36 us -> 7.16 us  [the longest x1 4.08 us: convolve_all(): fields = jnp.einsum('nkry,nkyz->nrz', smooth, mixed, precision=mxu_value)]
    psum x1 -> x0, blocking collectives: 22.9 us -> none  [shards(): visit_count, visit_load = lax.psum((local_count, local_load), 'patch')]
    all_to_all x3 -> x1, waiting for transfers between devices: 6.63 us -> 26.5 us  [shards(): lax.all_to_all(payload, 'patch', split_axis=0, concat_axis=0, tiled=True)]
    scatter x3, local copies, waits for them, and re-layouts: 13.6 us -> 0.72 us  [the longest x1 0.45 us: shards(): meta.at[:, 4, :VISITS].set(jnp.broadcast_to(local_load, (devices, VISITS)))]
    all_to_all x3 -> x1, starting transfers between devices: 17 us -> 7.31 us  [shards(): lax.all_to_all(payload, 'patch', split_axis=0, concat_axis=0, tiled=True)]
    dot_general x6 -> x0, local copies, waits for them, and re-layouts: 8.72 us -> none  [convolve(): jnp.einsum('nkp,npid->nkid', kernel_split[:, gauss_index], poly_planes, p...]
    another operation x18 -> x4, local copies, waits for them, and re-layouts: 5.34 us -> 0.2 us  [the longest x1 0.11 us: convolve_all(): jnp.stack([c[0] + c[1] * x_line + c[3] * (x_line * x_line), c[2] + c[4] *...]
    reduce_sum x0 -> x1, local copies, waits for them, and re-layouts: none -> 3.31 us  [convolve_all(): jnp.sum(col_ops[None, :, None, :, :, None, :] * fx[:, :, :, :, None, :, :...]
  transfers between devices with their start and end apart: 3 -> 1, of which waited for: 1 -> 1; matrix products, arithmetic and copies ran while one was open for 55% -> 0% of each run, Pallas kernels for 0% -> 0%
where the time goes in v1:
time: 93.3 us; the launch traced here: 92.9 us
  waiting for transfers between devices  26.5 us (28%)
  other arithmetic  25.6 us (27%)
  matrix products  24.6 us (26%)
  local copies, waits for them, and re-layouts  7.52 us (8%)
  starting transfers between devices  7.31 us (8%)
  between operations  1.13 us (1%)
    all_to_all x1, waiting for transfers between devices, shards(): lax.all_to_all(payload, 'patch', split_axis=0, concat_axis=0, tiled=True)  26.5 us
    dot_general x8, matrix products, place_group(): jnp.einsum('vmwn,vny->vmwy', pixel_block_tile, column_selection, precisio...  11.7 us
    all_to_all x1, starting transfers between devices, shards(): lax.all_to_all(payload, 'patch', split_axis=0, concat_axis=0, tiled=True)  7.31 us
    mul x6, other arithmetic, tap_values(): jnp.exp(-offsets * offsets / (2.0 * spread * spread)) / gauss_total * inside  6.97 us
    mul x6, other arithmetic, tap_values(): profile * scaled  6.63 us
    dot_general x8, matrix products, place_group(): jnp.einsum('gri,gkip->krp', row_select, broadened_width, precision=larges...  5.76 us
    dot_general x1, matrix products, convolve_all(): fields = jnp.einsum('nkry,nkyz->nrz', smooth, mixed, precision=mxu_value)  4.08 us
    reduce_sum x1, local copies, waits for them, and re-layouts, convolve_all(): jnp.sum(col_ops[None, :, None, :, :, None, :] * fx[:, :, :, :, None, :, :...  3.31 us
  transfers between devices with their start and end apart: 1, of which 1 were waited for; matrix products, arithmetic and copies ran while one was open for 0% of the time, Pallas kernels for 0%

profile of v1, /device:TPU:0, one launch (start us, length us, event | category | flops | bytes accessed | tf_op | source)
XLA Modules:
  0.0 92.9 jit_solution(15024950080672934833)
XLA Ops:
  0.7 0.7 exponential_reduce_fusion.2
  1.3 0.7 divide_select_fusion.5
  2.1 0.7 fusion.40
  2.8 0.6 exponential_reduce_fusion.1
  3.4 0.7 divide_select_fusion.4
  4.1 0.7 fusion.42
  4.8 0.6 exponential_reduce_fusion
  5.4 0.7 divide_select_fusion.3
  6.1 0.7 fusion.38
  6.8 1.6 %divide_select_fusion.2 = (f32[1,256,276]{1,2,0:T(8,128)}, f32[1,256,276]{1,2,0:T(8,128)}) fusion(f32[]{:T(128)} %exponential_reduce_fusion.2), kind=kLoop, calls=%fused_computation.40 | loop fusion | flops 918528 | bytes 565252 | tf_op jit(solution)/shard_map/mul | solution.py:25
  8.5 1.5 %fusion.30 = f32[1,256,276]{1,2,0:T(8,128)} fusion(f32[]{:T(128)} %exponential_reduce_fusion.2), kind=kLoop, calls=%fused_computation.49 | loop fusion | flops 847872 | bytes 282628 | tf_op jit(solution)/shard_map/mul | solution.py:27
  10.0 1.6 %divide_select_fusion.1 = (f32[1,256,276]{1,2,0:T(8,128)}, f32[1,256,276]{1,2,0:T(8,128)}) fusion(f32[]{:T(128)} %exponential_reduce_fusion.1), kind=kLoop, calls=%fused_computation.39 | loop fusion | flops 918528 | bytes 565252 | tf_op jit(solution)/shard_map/mul | solution.py:25
  11.6 1.5 %fusion.32 = f32[1,256,276]{1,2,0:T(8,128)} fusion(f32[]{:T(128)} %exponential_reduce_fusion.1), kind=kLoop, calls=%fused_computation.51 | loop fusion | flops 847872 | bytes 282628 | tf_op jit(solution)/shard_map/mul | solution.py:27
  13.1 1.6 %divide_select_fusion = (f32[1,256,276]{1,2,0:T(8,128)}, f32[1,256,276]{1,2,0:T(8,128)}) fusion(f32[]{:T(128)} %exponential_reduce_fusion), kind=kLoop, calls=%fused_computation.38 | loop fusion | flops 918528 | bytes 565252 | tf_op jit(solution)/shard_map/mul | solution.py:25
  14.7 1.5 %fusion.28 = f32[1,256,276]{1,2,0:T(8,128)} fusion(f32[]{:T(128)} %exponential_reduce_fusion), kind=kLoop, calls=%fused_computation.47 | loop fusion | flops 847872 | bytes 282628 | tf_op jit(solution)/shard_map/mul | solution.py:27
  16.2 0.1 copy.68
  16.3 0.2 fusion.57
  16.5 0.2 copy.69
  16.8 0.2 copy.71
  17.0 0.2 copy.73
  17.2 0.2 copy.75
  17.5 0.2 copy.77
  17.7 0.2 copy.79
  17.9 0.4 multiply_add_fusion.1
  18.3 0.1 stack_broadcast_in_dim.2
  18.6 2.7 %multiply_reduce_fusion = f32[2,3,3,128,3,128]{5,3,4,2,1,0:T(8,128)} fusion(f32[2,3,3,3,3,128]{5,4,3,2,1,0:T(4,128)S(1)} %pad_maximum_fusion.4, f32[3,3,128,128]{3,2,1,0:T(8,128)S(1)} %pad_maximum_fusion.2), kind=kLoop, calls=%fused_computation.20 | loop fusion | flops 4423680 | bytes 4211712 | tf_op jit(solution)/shard_map/reduce_sum | solution.py:62
  21.3 3.3 %copy.81 = f32[2,3,3,128,3,128]{3,5,4,2,1,0:T(8,128)S(1)} copy(f32[2,3,3,128,3,128]{5,3,4,2,1,0:T(8,128)} %multiply_reduce_fusion) | data formatting | bytes 7077888 | tf_op jit(solution)/shard_map/reduce_sum | solution.py:62
  24.7 1.3 %maximum_bitcast_fusion = f32[1,3,256,276]{2,3,1,0:T(8,128)S(1)} fusion(f32[1,256,276]{1,2,0:T(8,128)} %get-tuple-element.195, f32[1,256,276]{1,2,0:T(8,128)} %fusion.30, f32[1,256,276]{1,2,0:T(8,128)} %get-tuple-element.194), kind=kLoop, calls=%fused_computation.26 | loop fusion | flops 423936 | bytes 1695744 | tf_op jit(solution)/shard_map/stack | solution.py:28
  26.0 1.2 %maximum_bitcast_fusion.1 = f32[1,3,256,276]{2,3,1,0:T(8,128)S(1)} fusion(f32[1,256,276]{1,2,0:T(8,128)} %get-tuple-element.191, f32[1,256,276]{1,2,0:T(8,128)} %fusion.32, f32[1,256,276]{1,2,0:T(8,128)} %get-tuple-element.190), kind=kLoop, calls=%fused_computation.27 | loop fusion | flops 423936 | bytes 1695744 | tf_op jit(solution)/shard_map/stack | solution.py:28
  27.3 0.2 pad_maximum_fusion
  27.5 0.7 copy-done.3
  28.2 2.2 %fusion.25 = f32[2,128,9,256]{3,1,2,0:T(8,128)S(1)} fusion(f32[9,256,276,1]{1,2,0,3:T(8,128)S(1)} %bitcast.103, f32[2,256,128]{2,1,0:T(8,128)S(1)} %copy-done.3), kind=kOutput, calls=%fused_computation.36 | convolution fusion | flops 976748544 | bytes 5165056 | tf_op jit(solution)/shard_map/krj,njx->nkrx/dot_general | solution.py:49
  30.5 4.1 %fusion.19 = f32[2,256,384]{2,1,0:T(8,128)S(1)} fusion(f32[2,9,128,384]{2,3,1,0:T(8,128)S(1)} %bitcast.102, f32[2,128,9,256]{3,1,2,0:T(8,128)S(1)} %fusion.25), kind=kOutput, calls=%fused_computation.24 | convolution fusion | flops 1358954496 | bytes 6684672 | tf_op jit(solution)/shard_map/nkry,nkyz->nrz/dot_general | solution.py:66
  34.6 0.1 fusion.35
  34.8 0.2 convert_reduce_fusion.1
  35.1 0.7 fusion.22
  35.8 0.2 reshape.602
  36.0 0.2 select_reduce_fusion
  36.3 0.1 fusion.43
  36.7 0.3 scatter.11
  37.0 0.4 scatter.14
  37.4 1.1 %pad_maximum_fusion.1 = f32[8,264,128]{2,1,0:T(8,128)} fusion(f32[8,8,128]{2,1,0:T(8,128)S(1)} %scatter.14, f32[8,256,128]{2,1,0:T(8,128)S(1)} %reshape.602), kind=kLoop, calls=%fused_computation.25 | loop fusion | flops 270336 | bytes 2162688 | tf_op jit(solution)/shard_map/concatenate | solution.py:154
  38.5 7.3 %all-to-all-start = ((f32[8,264,128]{2,1,0:T(8,128)}), f32[8,264,128]{2,1,0:T(8,128)S(1)}, u32[]{:S(2)}, u32[]{:S(2)}) async-start(f32[8,264,128]{2,1,0:T(8,128)} %pad_maximum_fusion.1), calls=%async_computation | async-start | bytes 2162688 | tf_op jit(solution)/shard_map/all_to_all | solution.py:155
  45.8 26.5 %all-to-all-done = f32[8,264,128]{2,1,0:T(8,128)S(1)} async-done(((f32[8,264,128]{2,1,0:T(8,128)}), f32[8,264,128]{2,1,0:T(8,128)S(1)}, u32[]{:S(2)}, u32[]{:S(2)}) %all-to-all-start) | async-done | bytes 1081376 | tf_op jit(solution)/shard_map/all_to_all | solution.py:155
  72.7 0.2 broadcast_multiply_fusion
  72.9 19.0 %while.16 = (s32[]{:T(128)}, f32[2,128,512]{1,2,0:T(8,128)S(1)}, f32[8,16,2,8,128]{4,3,2,1,0:T(8,128)S(1)}, s32[8,16,2]{1,0,2:T(8,128)S(1)}, s32[]{:T(128)}, /*index=5*/s32[]{:T(128)}) while((s32[]{:T(128)}, f32[2,128,512]{1,2,0:T(8,128)S(1)}, f32[8,16,2,8,128]{4,3,2,1,0:T(8,128)S(1)}, s32[8,16,2]{1,0,2:T(8,128)S(1)}, ...), condition=%wide.region_13.14_spmd.clone.clone, body=%wide.region_12.13_spmd.clone.clone.sunk | while | flops 403982464 | bytes 2246359 | solution.py:107
  73.0 1.5 %fusion.71 = f32[16,2,8,512]{3,2,1,0:T(8,128)S(1)} fusion(s32[16,128]{1,0:T(8,128)S(1)} %iota_add_fusion.4, f32[8,16,2,8,128]{4,3,2,1,0:T(8,128)S(1)} %get-tuple-element.243, s32[]{:T(128)} %get-tuple-element.235), kind=kOutput, calls=%fused_computation.5.clone.1 | convolution fusion | flops 202375168 | bytes 663556 | tf_op jit(solution)/shard_map/while/body/eval_jaxpr/vmwn,vny->vmwy/dot_general | solution.py:97
  74.6 0.7 fusion.72
  75.4 1.5 %fusion.71 = f32[16,2,8,512]{3,2,1,0:T(8,128)S(1)} fusion(s32[16,128]{1,0:T(8,128)S(1)} %iota_add_fusion.4, f32[8,16,2,8,128]{4,3,2,1,0:T(8,128)S(1)} %get-tuple-element.243, s32[]{:T(128)} %get-tuple-element.235), kind=kOutput, calls=%fused_computation.5.clone.1 | convolution fusion | flops 202375168 | bytes 663556 | tf_op jit(solution)/shard_map/while/body/eval_jaxpr/vmwn,vny->vmwy/dot_general | solution.py:97
  76.9 0.7 fusion.72
  77.8 1.5 %fusion.71 = f32[16,2,8,512]{3,2,1,0:T(8,128)S(1)} fusion(s32[16,128]{1,0:T(8,128)S(1)} %iota_add_fusion.4, f32[8,16,2,8,128]{4,3,2,1,0:T(8,128)S(1)} %get-tuple-element.243, s32[]{:T(128)} %get-tuple-element.235), kind=kOutput, calls=%fused_computation.5.clone.1 | convolution fusion | flops 202375168 | bytes 663556 | tf_op jit(solution)/shard_map/while/body/eval_jaxpr/vmwn,vny->vmwy/dot_general | solution.py:97
  79.3 0.7 fusion.72
  80.1 1.5 %fusion.71 = f32[16,2,8,512]{3,2,1,0:T(8,128)S(1)} fusion(s32[16,128]{1,0:T(8,128)S(1)} %iota_add_fusion.4, f32[8,16,2,8,128]{4,3,2,1,0:T(8,128)S(1)} %get-tuple-element.243, s32[]{:T(128)} %get-tuple-element.235), kind=kOutput, calls=%fused_computation.5.clone.1 | convolution fusion | flops 202375168 | bytes 663556 | tf_op jit(solution)/shard_map/while/body/eval_jaxpr/vmwn,vny->vmwy/dot_general | solution.py:97
  81.7 0.7 fusion.72
  82.5 1.5 %fusion.71 = f32[16,2,8,512]{3,2,1,0:T(8,128)S(1)} fusion(s32[16,128]{1,0:T(8,128)S(1)} %iota_add_fusion.4, f32[8,16,2,8,128]{4,3,2,1,0:T(8,128)S(1)} %get-tuple-element.243, s32[]{:T(128)} %get-tuple-element.235), kind=kOutput, calls=%fused_computation.5.clone.1 | convolution fusion | flops 202375168 | bytes 663556 | tf_op jit(solution)/shard_map/while/body/eval_jaxpr/vmwn,vny->vmwy/dot_general | solution.py:97
  84.0 0.7 fusion.72
  84.9 1.5 %fusion.71 = f32[16,2,8,512]{3,2,1,0:T(8,128)S(1)} fusion(s32[16,128]{1,0:T(8,128)S(1)} %iota_add_fusion.4, f32[8,16,2,8,128]{4,3,2,1,0:T(8,128)S(1)} %get-tuple-element.243, s32[]{:T(128)} %get-tuple-element.235), kind=kOutput, calls=%fused_computation.5.clone.1 | convolution fusion | flops 202375168 | bytes 663556 | tf_op jit(solution)/shard_map/while/body/eval_jaxpr/vmwn,vny->vmwy/dot_general | solution.py:97
  86.4 0.7 fusion.72
  87.3 1.5 %fusion.71 = f32[16,2,8,512]{3,2,1,0:T(8,128)S(1)} fusion(s32[16,128]{1,0:T(8,128)S(1)} %iota_add_fusion.4, f32[8,16,2,8,128]{4,3,2,1,0:T(8,128)S(1)} %get-tuple-element.243, s32[]{:T(128)} %get-tuple-element.235), kind=kOutput, calls=%fused_computation.5.clone.1 | convolution fusion | flops 202375168 | bytes 663556 | tf_op jit(solution)/shard_map/while/body/eval_jaxpr/vmwn,vny->vmwy/dot_general | solution.py:97
  88.8 0.7 fusion.72
  89.6 1.5 %fusion.71 = f32[16,2,8,512]{3,2,1,0:T(8,128)S(1)} fusion(s32[16,128]{1,0:T(8,128)S(1)} %iota_add_fusion.4, f32[8,16,2,8,128]{4,3,2,1,0:T(8,128)S(1)} %get-tuple-element.243, s32[]{:T(128)} %get-tuple-element.235), kind=kOutput, calls=%fused_computation.5.clone.1 | convolution fusion | flops 202375168 | bytes 663556 | tf_op jit(solution)/shard_map/while/body/eval_jaxpr/vmwn,vny->vmwy/dot_general | solution.py:97
  91.2 0.7 fusion.72
  91.9 0.2 copy.88
  92.1 0.8 slice_divide_fusion
  (90 shorter events, 2.4 us)
Async XLA Ops:
  0.6 15.6 %copy-start.6 = (f32[2,27,6]{1,0,2:T(2,128)S(1)}, f32[2,27,6]{1,0,2:T(2,128)}, u32[]{:S(2)}) copy-start(f32[2,27,6]{1,0,2:T(2,128)} %param.19) | copy-start | bytes 3892
  24.6 2.5 %copy-start = (f32[1,256,276]{1,2,0:T(8,128)S(1)}, f32[1,256,276]{1,2,0:T(8,128)}, u32[]{:S(2)}) copy-start(f32[1,256,276]{1,2,0:T(8,128)} %fusion.28) | copy-start | bytes 847876
  24.7 2.5 %copy-start.1 = (f32[1,256,276]{1,2,0:T(8,128)S(1)}, f32[1,256,276]{1,2,0:T(8,128)}, u32[]{:S(2)}) copy-start(f32[1,256,276]{1,2,0:T(8,128)} %get-tuple-element.186) | copy-start | bytes 847876
  24.7 2.5 %copy-start.2 = (f32[1,256,276]{1,2,0:T(8,128)S(1)}, f32[1,256,276]{1,2,0:T(8,128)}, u32[]{:S(2)}) copy-start(f32[1,256,276]{1,2,0:T(8,128)} %get-tuple-element.187) | copy-start | bytes 847876
  27.3 1.0 %copy-start.3 = (f32[2,256,128]{2,1,0:T(8,128)S(1)}, f32[2,256,128]{2,1,0:T(8,128)}, u32[]{:S(2)}) copy-start(f32[2,256,128]{2,1,0:T(8,128)} %param.16) | copy-start | bytes 786436
  30.5 4.1 %copy-start.5 = (s32[2,256,128]{2,1,0:T(8,128)S(1)}, s32[2,256,128]{2,1,0:T(8,128)}, u32[]{:S(2)}) copy-start(s32[2,256,128]{2,1,0:T(8,128)} %param.18) | copy-start | bytes 786436
  30.5 4.3 %copy-start.8 = (s32[64,1]{0,1:T(1,128)S(1)}, s32[64,1]{0,1:T(1,128)}, u32[]{:S(2)}) copy-start(s32[64,1]{0,1:T(1,128)} %param.21) | copy-start | bytes 772
  34.7 1.2 %copy-start.4 = (f32[2,256,128]{2,1,0:T(8,128)S(1)}, f32[2,256,128]{2,1,0:T(8,128)}, u32[]{:S(2)}) copy-start(f32[2,256,128]{2,1,0:T(8,128)} %param.17) | copy-start | bytes 786436
  34.8 1.4 %copy-start.7 = (s32[2,1]{0,1:T(1,128)S(1)}, s32[2,1]{0,1:T(1,128)}, u32[]{:S(2)}) copy-start(s32[2,1]{0,1:T(1,128)} %param.20) | copy-start | bytes 28
  34.8 1.5 %copy-start.9 = (s32[64]{0:T(128)S(1)}, s32[64]{0:T(128)}, u32[]{:S(2)}) copy-start(s32[64]{0:T(128)} %param.23) | copy-start | bytes 772
  34.8 1.5 %copy-start.10 = (s32[64]{0:T(128)S(1)}, s32[64]{0:T(128)}, u32[]{:S(2)}) copy-start(s32[64]{0:T(128)} %param.22) | copy-start | bytes 772
  38.5 33.8 %all-to-all-start = ((f32[8,264,128]{2,1,0:T(8,128)}), f32[8,264,128]{2,1,0:T(8,128)S(1)}, u32[]{:S(2)}, u32[]{:S(2)}) async-start(f32[8,264,128]{2,1,0:T(8,128)} %pad_maximum_fusion.1), calls=%async_computation | async-start | bytes 2162688 | tf_op jit(solution)/shard_map/all_to_all | solution.py:155

commit v2 on v1

--- a/solution.py
+++ b/solution.py
@@ -1,6 +1,7 @@
 import math
 
 import jax
+import numpy as np
 import jax.numpy as jnp
 from jax import lax
 from jax.sharding import PartitionSpec as P
@@ -16,38 +17,52 @@
 mxu_value = lax.Precision.HIGH
 
 
-def tap_values(offsets, kernel_half_width):
-    support = jnp.arange(-kernel_half_width, kernel_half_width + 1).astype(jnp.float32)
-    inside = (jnp.abs(offsets) <= kernel_half_width).astype(jnp.float32)
+def tap_table(kernel_half_width):
+    support = np.arange(-kernel_half_width, kernel_half_width + 1).astype(np.float64)
     tables = []
     for spread in gauss_widths:
-        gauss_total = jnp.sum(jnp.exp(-support * support / (2.0 * spread * spread)))
-        profile = jnp.exp(-offsets * offsets / (2.0 * spread * spread)) / gauss_total * inside
-        scaled = offsets / spread
-        tables.append(jnp.stack([profile, profile * scaled, profile * scaled * scaled]))
-    return jnp.stack(tables)
-
-
-def row_filters(row_count, kernel_half_width):
-    row_ids = jnp.arange(row_count)[:, None]
-    window_ids = jnp.arange(row_count + 2 * kernel_half_width)[None, :]
-    return tap_values(
-        (window_ids - row_ids - kernel_half_width).astype(jnp.float32), kernel_half_width
-    )
-
-
-def column_filters(column_count, kernel_half_width):
-    source = jnp.arange(column_count)[:, None]
-    target_patch = jnp.arange(column_count)[None, :]
-    return tap_values((source - target_patch).astype(jnp.float32), kernel_half_width)
-
-
-def convolve_all(padded, kernel_coeffs, height):
+        s32 = float(np.float32(spread))
+        gauss_total = np.sum(np.exp(-support * support / (2.0 * s32 * s32)))
+        profile = np.exp(-support * support / (2.0 * s32 * s32)) / gauss_total
+        scaled = support / s32
+        tables.append(np.stack([profile, profile * scaled, profile * scaled * scaled]))
+    return np.stack(tables)
+
+
+def row_blocks(block_rows, window_rows, kernel_half_width):
+    taps = tap_table(kernel_half_width).reshape(9, 2 * kernel_half_width + 1)
+    out = np.zeros((9, block_rows, window_rows), np.float64)
+    for i in range(block_rows):
+        out[:, i, i : i + 2 * kernel_half_width + 1] = taps
+    return out.astype(np.float32)
+
+
+def column_ops(column_count, kernel_half_width):
+    taps = tap_table(kernel_half_width)
+    out = np.zeros((3, 3, column_count, column_count), np.float64)
+    for y in range(column_count):
+        lo = max(0, y - kernel_half_width)
+        hi = min(column_count, y + kernel_half_width + 1)
+        for x in range(lo, hi):
+            out[:, :, y, x] = taps[:, :, y - x + kernel_half_width]
+    return out.astype(np.float32)
+
+
+def convolve_all(exposures, kernel_coeffs):
     kernel_half_width = KS // 2
-    n, _, columns = padded.shape
-    rows = row_filters(height, kernel_half_width).reshape(9, height, height + 2 * kernel_half_width)
-    smooth = jnp.einsum("krj,njx->nkrx", rows, padded, precision=mxu_value)
-    col_ops = column_filters(columns, kernel_half_width)
+    n, height, columns = exposures.shape
+    block = 8
+    blocks = height // block
+    span = 2 * kernel_half_width + block
+    reach = -(-span // block)
+    total_rows = (blocks + reach - 1) * block
+    padded = jnp.pad(
+        exposures, ((0, 0), (kernel_half_width, total_rows - height - kernel_half_width), (0, 0))
+    ).reshape(n, blocks + reach - 1, block, columns)
+    windows = jnp.concatenate([padded[:, j : j + blocks] for j in range(reach)], axis=2)
+    rows = jnp.asarray(row_blocks(block, reach * block, kernel_half_width))
+    smooth = jnp.einsum("kit,nqtx->nqkix", rows, windows, precision=mxu_value)
+    col_ops = jnp.asarray(column_ops(columns, kernel_half_width))
     x_line = 2.0 * jnp.arange(columns).astype(jnp.float32) / (columns - 1) - 1.0
     coef = kernel_coeffs.reshape(n, 3, 3, 3, 6)
     c = [coef[..., p, None] for p in range(6)]
@@ -63,7 +78,8 @@
         col_ops[None, :, None, :, :, None, :] * fx[:, :, :, :, None, :, :], axis=3
     )
     mixed = mixed.reshape(n, 9, columns, 3 * columns)
-    fields = jnp.einsum("nkry,nkyz->nrz", smooth, mixed, precision=mxu_value)
+    fields = jnp.einsum("nqkiy,nkyz->nqiz", smooth, mixed, precision=mxu_value)
+    fields = fields.reshape(n, height, 3 * columns)
     y_line = (2.0 * jnp.arange(height).astype(jnp.float32) / (height - 1) - 1.0)[None, :, None]
     return (
         fields[:, :, :columns]
@@ -117,7 +133,6 @@
     strip_rows = height // per_ccd
     devices = lax.axis_size("patch")
     capacity = 2 * strip_total // devices
-    kernel_half_width = KS // 2
     usable = (jnp.bitwise_and(mask_bits, 3) != 3).astype(jnp.float32)
     visit_hot = (ccd_visit == jnp.arange(VISITS)[None, :]).astype(jnp.float32)
     local_count = jnp.sum(jnp.sum(usable, axis=(1, 2))[:, None] * visit_hot, axis=0)
@@ -132,18 +147,6 @@
     slot_total = devices * capacity
     chooser = (slot_index[None, :] == jnp.arange(slot_total)[:, None]).astype(jnp.float32)
 
-    padded = jnp.pad(exposures, ((0, 0), (kernel_half_width, kernel_half_width), (0, 0)))
-    convolved = convolve_all(padded, kernel_coeffs, height)
-    tiles = jnp.concatenate(
-        [
-            (usable * convolved).reshape(strip_total, strip_rows, columns),
-            usable.reshape(strip_total, strip_rows, columns),
-        ],
-        axis=1,
-    ).reshape(strip_total, 2 * strip_rows * columns)
-    packed = jnp.dot(chooser, tiles, precision=largest_value).reshape(
-        devices, capacity * 2 * strip_rows, columns
-    )
     strip_visit = jnp.repeat(ccd_visit[:, 0], per_ccd)
     placement = jnp.stack([strip_row, strip_col, strip_visit], axis=1).astype(jnp.float32)
     slot_meta = jnp.dot(chooser, placement, precision=largest_value).reshape(devices, capacity, 3)
@@ -151,10 +154,22 @@
     meta = meta.at[:, 0:3, :capacity].set(jnp.swapaxes(slot_meta, 1, 2))
     meta = meta.at[:, 3, :VISITS].set(jnp.broadcast_to(local_count, (devices, VISITS)))
     meta = meta.at[:, 4, :VISITS].set(jnp.broadcast_to(local_load, (devices, VISITS)))
-    payload = jnp.concatenate([packed, meta], axis=1)
-    got = lax.all_to_all(payload, "patch", split_axis=0, concat_axis=0, tiled=True)
-    body_rows = capacity * 2 * strip_rows
-    got_meta = got[:, body_rows:, :]
+    body_rows = capacity * strip_rows
+    weight_tiles = usable.reshape(strip_total, strip_rows * columns)
+    weight_packed = jnp.dot(chooser, weight_tiles, precision=largest_value).reshape(
+        devices, body_rows, columns
+    )
+    first = jnp.concatenate([weight_packed, meta], axis=1)
+    got_first = lax.all_to_all(first, "patch", split_axis=0, concat_axis=0, tiled=True)
+
+    convolved = convolve_all(exposures, kernel_coeffs)
+    flux_tiles = (usable * convolved).reshape(strip_total, strip_rows * columns)
+    flux_packed = jnp.dot(chooser, flux_tiles, precision=largest_value).reshape(
+        devices, body_rows, columns
+    )
+    got_flux = lax.all_to_all(flux_packed, "patch", split_axis=0, concat_axis=0, tiled=True)
+
+    got_meta = got_first[:, body_rows:, :]
     visit_count = jnp.sum(got_meta[:, 3, :VISITS], axis=0)
     visit_load = jnp.sum(got_meta[:, 4, :VISITS], axis=0)
     visit_weight = (visit_count + 1.0) / (visit_load + 1.0)
@@ -163,10 +178,12 @@
     slot_visit = got_meta[:, 2, :capacity].reshape(slot_total).astype(jnp.int32)
     slot_hot = (slot_visit[:, None] == jnp.arange(VISITS)[None, :]).astype(jnp.float32)
     slot_weight = jnp.sum(slot_hot * visit_weight[None, :], axis=1)
-    body = got[:, :body_rows, :].reshape(slot_total, 2, strip_rows, columns)
-    body = body * slot_weight[:, None, None, None]
+    weight_body = got_first[:, :body_rows, :].reshape(slot_total, strip_rows, columns)
+    flux_body = got_flux.reshape(slot_total, strip_rows, columns)
+    weight_body = weight_body * slot_weight[:, None, None]
+    flux_body = flux_body * slot_weight[:, None, None]
     offsets = jnp.stack([slot_rows, slot_cols], axis=1)
-    numerator, weight_map = place_slots(body[:, 0], body[:, 1], offsets, PH, PW)
+    numerator, weight_map = place_slots(flux_body, weight_body, offsets, PH, PW)
     coadd_image = numerator / jnp.maximum(weight_map, 1.0)
     return (coadd_image[None], weight_map[None])
 

time: 93.3 us -> 82.4 us (0.88)
  other arithmetic: 25.6 us -> 9.37 us
  starting transfers between devices: 7.31 us -> 10.9 us
  matrix products: 24.6 us -> 22.9 us
  waiting for transfers between devices: 26.5 us -> 28.2 us
  local copies, waits for them, and re-layouts: 7.52 us -> 9.19 us
    mul x14 -> x2, other arithmetic: 13.9 us -> 0.35 us  [the longest x1 0.21 us: shards(): flux_body = flux_body * slot_weight[:, None, None]]
    all_to_all x1 -> x2, starting transfers between devices: 7.31 us -> 10.9 us  [the longest x1 7.31 us: shards(): lax.all_to_all(first, 'patch', split_axis=0, concat_axis=0, tiled=True)]
    another operation x8 -> x1, other arithmetic: 2.88 us -> 0.07 us  [place_slots(): jnp.stack([flux_flat, weight_flat], axis=1)]
    dot_general x3 -> x4, matrix products: 7.04 us -> 4.69 us  [the longest x1 2.27 us: convolve_all(): fields = jnp.einsum('nqkiy,nkyz->nqiz', smooth, mixed, precision=mxu_value)]
    reduce_sum x3 -> x0, other arithmetic: 1.93 us -> none  [tap_values(): gauss_total = jnp.sum(jnp.exp(-support * support / (2.0 * spread * spread)))]
    reshape x1 -> x5, local copies, waits for them, and re-layouts: 0.16 us -> 2.05 us  [the longest x1 0.98 us: convolve_all(): padded = jnp.pad(exposures, ((0, 0), (kernel_half_width, total_rows - hei...]
    all_to_all x1 -> x2, waiting for transfers between devices: 26.5 us -> 28.2 us  [the longest x1 14.3 us: shards(): lax.all_to_all(flux_packed, 'patch', split_axis=0, concat_axis=0, tiled=T...]
    reduce_sum x1, other arithmetic: 2.74 us -> 4.17 us  [convolve_all(): jnp.sum(col_ops[None, :, None, :, :, None, :] * fx[:, :, :, :, None, :, :...]
  transfers between devices with their start and end apart: 1 -> 2, of which waited for: 1 -> 2; matrix products, arithmetic and copies ran while one was open for 0% -> 2% of each run, Pallas kernels for 0% -> 0%
where the time goes in v2:
time: 82.4 us; the launch traced here: 81.9 us
  waiting for transfers between devices  28.2 us (34%)
  matrix products  22.9 us (28%)
  starting transfers between devices  10.9 us (13%)
  other arithmetic  9.37 us (11%)
  local copies, waits for them, and re-layouts  9.19 us (11%)
  between operations  0.95 us (1%)
    all_to_all x1, waiting for transfers between devices, shards(): lax.all_to_all(flux_packed, 'patch', split_axis=0, concat_axis=0, tiled=T...  14.3 us
    all_to_all x1, waiting for transfers between devices, shards(): lax.all_to_all(first, 'patch', split_axis=0, concat_axis=0, tiled=True)  13.9 us
    dot_general x8, matrix products, place_group(): jnp.einsum('vmwn,vny->vmwy', pixel_block_tile, column_selection, precisio...  11.7 us
    all_to_all x1, starting transfers between devices, shards(): lax.all_to_all(first, 'patch', split_axis=0, concat_axis=0, tiled=True)  7.31 us
    dot_general x8, matrix products, place_group(): jnp.einsum('gri,gkip->krp', row_select, broadened_width, precision=larges...  5.76 us
    reduce_sum x1, other arithmetic, convolve_all(): jnp.sum(col_ops[None, :, None, :, :, None, :] * fx[:, :, :, :, None, :, :...  4.17 us
    all_to_all x1, starting transfers between devices, shards(): lax.all_to_all(flux_packed, 'patch', split_axis=0, concat_axis=0, tiled=T...  3.64 us
    reduce_sum x1, local copies, waits for them, and re-layouts, convolve_all(): jnp.sum(col_ops[None, :, None, :, :, None, :] * fx[:, :, :, :, None, :, :...  3.31 us
  transfers between devices with their start and end apart: 2, of which 2 were waited for; matrix products, arithmetic and copies ran while one was open for 2% of the time, Pallas kernels for 0%

profile of v2, /device:TPU:0, one launch (start us, length us, event | category | flops | bytes accessed | tf_op | source)
XLA Modules:
  0.0 81.9 jit_solution(7379162448762953336)
XLA Ops:
  0.7 0.8 copy.70
  1.4 0.2 fusion.51
  1.7 0.2 copy.71
  1.9 0.2 copy.73
  2.1 0.2 copy.75
  2.3 0.2 copy.77
  2.6 0.2 copy.79
  2.8 0.2 copy.81
  3.0 0.4 multiply_add_fusion.1
  3.4 0.1 stack_broadcast_in_dim.2
  3.5 0.1 pad_maximum_fusion.2
  3.6 4.2 %multiply_reduce_fusion = f32[2,3,3,128,3,128]{5,3,4,2,1,0:T(8,128)} fusion(f32[2,3,3,3,3,128]{5,4,3,2,1,0:T(4,128)S(1)} %pad_maximum_fusion.2, f32[3,3,128,128]{3,2,1,0:T(8,128)} %constant.143.clone), kind=kLoop, calls=%fused_computation.20 | loop fusion | flops 4423680 | bytes 4211712 | tf_op jit(solution)/shard_map/reduce_sum | solution.py:77
  7.8 3.3 %copy.83 = f32[2,3,3,128,3,128]{3,5,4,2,1,0:T(8,128)S(1)} copy(f32[2,3,3,128,3,128]{5,3,4,2,1,0:T(8,128)} %multiply_reduce_fusion) | data formatting | bytes 7077888 | tf_op jit(solution)/shard_map/reduce_sum | solution.py:77
  11.1 1.0 %pad_bitcast_fusion = f32[2,35,8,128]{3,2,1,0:T(8,128)S(1)} fusion(f32[2,256,128]{2,1,0:T(8,128)} %param.18), kind=kLoop, calls=%fused_computation.37 | loop fusion | bytes 548864 | tf_op jit(solution)/shard_map/reshape | solution.py:61
  12.1 1.8 %fusion.22 = f32[2,32,128,9,8]{2,4,3,1,0:T(8,128)S(1)} fusion(f32[9,8,32,1,1]{2,1,0,4,3:T(8,128)} %constant.153, f32[2,32,8,128]{3,2,1,0:T(8,128)S(1)} %get-tuple-element.177, f32[2,32,8,128]{3,2,1,0:T(8,128)S(1)} %get-tuple-element.178, f32[2,32,8,128]{3,2,1,0:T(8,128)S(1)} %get-tuple-element.179, f32[2,32,8,128]{3,2,1,0:T(8,128)S(1)} %get-tuple-element.176), kind=kOutput, calls=%fused_computation.25 | convolution fusion | flops 114032640 | bytes 3417088 | tf_op jit(solution)/shard_map/kit,nqtx->nqkix/dot_general | solution.py:64
  14.0 2.3 %fusion.19 = f32[2,256,384]{2,1,0:T(8,128)S(1)} fusion(f32[2,9,128,384,1]{2,3,1,4,0:T(8,128)S(1)} %bitcast.101, f32[2,32,128,9,8]{2,4,3,1,0:T(8,128)S(1)} %fusion.22), kind=kOutput, calls=%fused_computation.23 | convolution fusion | flops 1358954496 | bytes 6684672 | tf_op jit(solution)/shard_map/nqkiy,nkyz->nqiz/dot_general | solution.py:81
  16.3 0.1 fusion.31
  16.4 0.1 reshape.331
  16.5 1.1 %select_reduce_fusion = (f32[2]{0:T(128)S(1)}, f32[2]{0:T(128)S(1)}) fusion(pred[2,256,128]{2,1,0:T(32,128)(4,1)S(1)} %get-tuple-element.171, f32[2,256,128]{2,1,0:T(8,128)} %param.19), kind=kLoop, calls=%fused_computation.44 | loop fusion | flops 262140 | bytes 327696 | tf_op jit(solution)/shard_map/reduce_sum | solution.py:139
  17.6 0.2 convert_reduce_fusion.1
  17.9 0.1 stack_reshape.3
  18.0 0.8 fusion.33
  18.8 0.1 reshape.333
  18.9 0.2 fusion.34
  19.2 0.1 reshape.332
  19.3 0.1 select_reduce_fusion.2
  19.4 0.3 scatter.11
  19.7 0.3 scatter.14
  19.9 0.8 %pad_maximum_fusion.1 = f32[8,136,128]{2,1,0:T(8,128)} fusion(f32[8,8,128]{2,1,0:T(8,128)S(1)} %scatter.14, f32[8,128,128]{2,1,0:T(8,128)S(1)} %reshape.332), kind=kLoop, calls=%fused_computation.33 | loop fusion | flops 139264 | bytes 1114112 | tf_op jit(solution)/shard_map/concatenate | solution.py:162
  20.8 7.3 %all-to-all-start.1 = ((f32[8,136,128]{2,1,0:T(8,128)}), f32[8,136,128]{2,1,0:T(8,128)S(1)}, u32[]{:S(2)}, u32[]{:S(2)}) async-start(f32[8,136,128]{2,1,0:T(8,128)} %pad_maximum_fusion.1), calls=%async_computation.1 | async-start | bytes 1114112 | tf_op jit(solution)/shard_map/all_to_all | solution.py:163
  28.1 0.4 fusion.35
  28.5 0.9 %reshape.329 = f32[8,128,128]{2,1,0:T(8,128)} reshape(f32[128,1024]{1,0:T(8,128)S(1)} %fusion.35) | data formatting | bytes 1048576 | tf_op jit(solution)/shard_map/reshape | solution.py:167
  29.4 13.9 %all-to-all-done.1 = f32[8,136,128]{2,1,0:T(8,128)S(1)} async-done(((f32[8,136,128]{2,1,0:T(8,128)}), f32[8,136,128]{2,1,0:T(8,128)S(1)}, u32[]{:S(2)}, u32[]{:S(2)}) %all-to-all-start.1) | async-done | bytes 557088 | tf_op jit(solution)/shard_map/all_to_all | solution.py:163
  43.3 3.6 %all-to-all-start = ((f32[8,128,128]{2,1,0:T(8,128)}), f32[8,128,128]{2,1,0:T(8,128)S(1)}, u32[]{:S(2)}, u32[]{:S(2)}) async-start(f32[8,128,128]{2,1,0:T(8,128)} %reshape.329), calls=%async_computation | async-start | bytes 1048576 | tf_op jit(solution)/shard_map/all_to_all | solution.py:170
  47.0 0.1 convert_element_type.88
  47.0 0.1 select_reduce_fusion.1
  47.1 0.1 mul.218
  47.3 14.3 %all-to-all-done = f32[8,128,128]{2,1,0:T(8,128)S(1)} async-done(((f32[8,128,128]{2,1,0:T(8,128)}), f32[8,128,128]{2,1,0:T(8,128)S(1)}, u32[]{:S(2)}, u32[]{:S(2)}) %all-to-all-start) | async-done | bytes 524320 | tf_op jit(solution)/shard_map/all_to_all | solution.py:170
  61.6 0.2 bitcast_multiply_fusion
  61.9 19.0 %while.16 = (s32[]{:T(128)}, f32[2,128,512]{1,2,0:T(8,128)S(1)}, f32[8,16,2,8,128]{4,3,2,1,0:T(8,128)S(1)}, s32[8,16,2]{1,0,2:T(8,128)S(1)}, s32[]{:T(128)}, /*index=5*/s32[]{:T(128)}) while((s32[]{:T(128)}, f32[2,128,512]{1,2,0:T(8,128)S(1)}, f32[8,16,2,8,128]{4,3,2,1,0:T(8,128)S(1)}, s32[8,16,2]{1,0,2:T(8,128)S(1)}, ...), condition=%wide.region_10.11_spmd.clone.clone, body=%wide.region_9.10_spmd.clone.clone.sunk | while | flops 403982464 | bytes 2246359 | solution.py:123
  61.9 0.1 iota_add_fusion.4
  62.0 1.5 %fusion.67 = f32[16,2,8,512]{3,2,1,0:T(8,128)S(1)} fusion(s32[16,128]{1,0:T(8,128)S(1)} %iota_add_fusion.4, f32[8,16,2,8,128]{4,3,2,1,0:T(8,128)S(1)} %get-tuple-element.237, s32[]{:T(128)} %get-tuple-element.229), kind=kOutput, calls=%fused_computation.5.clone.1 | convolution fusion | flops 202375168 | bytes 663556 | tf_op jit(solution)/shard_map/while/body/eval_jaxpr/vmwn,vny->vmwy/dot_general | solution.py:113
  63.5 0.7 fusion.68
  64.3 0.1 iota_add_fusion.4
  64.3 1.5 %fusion.67 = f32[16,2,8,512]{3,2,1,0:T(8,128)S(1)} fusion(s32[16,128]{1,0:T(8,128)S(1)} %iota_add_fusion.4, f32[8,16,2,8,128]{4,3,2,1,0:T(8,128)S(1)} %get-tuple-element.237, s32[]{:T(128)} %get-tuple-element.229), kind=kOutput, calls=%fused_computation.5.clone.1 | convolution fusion | flops 202375168 | bytes 663556 | tf_op jit(solution)/shard_map/while/body/eval_jaxpr/vmwn,vny->vmwy/dot_general | solution.py:113
  65.9 0.7 fusion.68
  66.6 0.1 iota_add_fusion.4
  66.7 1.5 %fusion.67 = f32[16,2,8,512]{3,2,1,0:T(8,128)S(1)} fusion(s32[16,128]{1,0:T(8,128)S(1)} %iota_add_fusion.4, f32[8,16,2,8,128]{4,3,2,1,0:T(8,128)S(1)} %get-tuple-element.237, s32[]{:T(128)} %get-tuple-element.229), kind=kOutput, calls=%fused_computation.5.clone.1 | convolution fusion | flops 202375168 | bytes 663556 | tf_op jit(solution)/shard_map/while/body/eval_jaxpr/vmwn,vny->vmwy/dot_general | solution.py:113
  68.3 0.7 fusion.68
  69.0 0.1 iota_add_fusion.4
  69.1 1.5 %fusion.67 = f32[16,2,8,512]{3,2,1,0:T(8,128)S(1)} fusion(s32[16,128]{1,0:T(8,128)S(1)} %iota_add_fusion.4, f32[8,16,2,8,128]{4,3,2,1,0:T(8,128)S(1)} %get-tuple-element.237, s32[]{:T(128)} %get-tuple-element.229), kind=kOutput, calls=%fused_computation.5.clone.1 | convolution fusion | flops 202375168 | bytes 663556 | tf_op jit(solution)/shard_map/while/body/eval_jaxpr/vmwn,vny->vmwy/dot_general | solution.py:113
  70.6 0.7 fusion.68
  71.4 0.1 iota_add_fusion.4
  71.5 1.5 %fusion.67 = f32[16,2,8,512]{3,2,1,0:T(8,128)S(1)} fusion(s32[16,128]{1,0:T(8,128)S(1)} %iota_add_fusion.4, f32[8,16,2,8,128]{4,3,2,1,0:T(8,128)S(1)} %get-tuple-element.237, s32[]{:T(128)} %get-tuple-element.229), kind=kOutput, calls=%fused_computation.5.clone.1 | convolution fusion | flops 202375168 | bytes 663556 | tf_op jit(solution)/shard_map/while/body/eval_jaxpr/vmwn,vny->vmwy/dot_general | solution.py:113
  73.0 0.7 fusion.68
  73.8 0.1 iota_add_fusion.4
  73.8 1.5 %fusion.67 = f32[16,2,8,512]{3,2,1,0:T(8,128)S(1)} fusion(s32[16,128]{1,0:T(8,128)S(1)} %iota_add_fusion.4, f32[8,16,2,8,128]{4,3,2,1,0:T(8,128)S(1)} %get-tuple-element.237, s32[]{:T(128)} %get-tuple-element.229), kind=kOutput, calls=%fused_computation.5.clone.1 | convolution fusion | flops 202375168 | bytes 663556 | tf_op jit(solution)/shard_map/while/body/eval_jaxpr/vmwn,vny->vmwy/dot_general | solution.py:113
  75.4 0.7 fusion.68
  76.2 1.5 %fusion.67 = f32[16,2,8,512]{3,2,1,0:T(8,128)S(1)} fusion(s32[16,128]{1,0:T(8,128)S(1)} %iota_add_fusion.4, f32[8,16,2,8,128]{4,3,2,1,0:T(8,128)S(1)} %get-tuple-element.237, s32[]{:T(128)} %get-tuple-element.229), kind=kOutput, calls=%fused_computation.5.clone.1 | convolution fusion | flops 202375168 | bytes 663556 | tf_op jit(solution)/shard_map/while/body/eval_jaxpr/vmwn,vny->vmwy/dot_general | solution.py:113
  77.7 0.7 fusion.68
  78.6 1.5 %fusion.67 = f32[16,2,8,512]{3,2,1,0:T(8,128)S(1)} fusion(s32[16,128]{1,0:T(8,128)S(1)} %iota_add_fusion.4, f32[8,16,2,8,128]{4,3,2,1,0:T(8,128)S(1)} %get-tuple-element.237, s32[]{:T(128)} %get-tuple-element.229), kind=kOutput, calls=%fused_computation.5.clone.1 | convolution fusion | flops 202375168 | bytes 663556 | tf_op jit(solution)/shard_map/while/body/eval_jaxpr/vmwn,vny->vmwy/dot_general | solution.py:113
  80.1 0.7 fusion.68
  80.9 0.2 copy.90
  81.1 0.8 slice_divide_fusion
  (57 shorter events, 1.2 us)
Async XLA Ops:
  14.0 2.3 %copy-start = (s32[2,256,128]{2,1,0:T(8,128)S(1)}, s32[2,256,128]{2,1,0:T(8,128)}, u32[]{:S(2)}) copy-start(s32[2,256,128]{2,1,0:T(8,128)} %param.20) | copy-start | bytes 786436
  14.0 3.7 %copy-start.2 = (s32[64,1]{0,1:T(1,128)S(1)}, s32[64,1]{0,1:T(1,128)}, u32[]{:S(2)}) copy-start(s32[64,1]{0,1:T(1,128)} %param.23) | copy-start | bytes 772
  14.0 3.8 %copy-start.1 = (s32[2,1]{0,1:T(1,128)S(1)}, s32[2,1]{0,1:T(1,128)}, u32[]{:S(2)}) copy-start(s32[2,1]{0,1:T(1,128)} %param.22) | copy-start | bytes 28
  20.8 22.5 %all-to-all-start.1 = ((f32[8,136,128]{2,1,0:T(8,128)}), f32[8,136,128]{2,1,0:T(8,128)S(1)}, u32[]{:S(2)}, u32[]{:S(2)}) async-start(f32[8,136,128]{2,1,0:T(8,128)} %pad_maximum_fusion.1), calls=%async_computation.1 | async-start | bytes 1114112 | tf_op jit(solution)/shard_map/all_to_all | solution.py:163
  43.3 18.3 %all-to-all-start = ((f32[8,128,128]{2,1,0:T(8,128)}), f32[8,128,128]{2,1,0:T(8,128)S(1)}, u32[]{:S(2)}, u32[]{:S(2)}) async-start(f32[8,128,128]{2,1,0:T(8,128)} %reshape.329), calls=%async_computation | async-start | bytes 1048576 | tf_op jit(solution)/shard_map/all_to_all | solution.py:170

commit v3 on v2

--- a/solution.py
+++ b/solution.py
@@ -1,9 +1,9 @@
-import math
-
 import jax
 import numpy as np
 import jax.numpy as jnp
 from jax import lax
+from jax.experimental import pallas as pl
+from jax.experimental.pallas import tpu as pltpu
 from jax.sharding import PartitionSpec as P
 
 PH = 128
@@ -88,40 +88,71 @@
     )
 
 
-def place_slots(flux_flat, weight_flat, offsets, patch_rows, patch_cols):
-    slot_total, strip_rows, columns = flux_flat.shape
-    group = math.gcd(slot_total, 16)
-    pairs = jnp.stack([flux_flat, weight_flat], axis=1).reshape(
-        slot_total // group, group, 2, strip_rows, columns
-    )
-    grouped_offsets = offsets.reshape(slot_total // group, group, offsets.shape[1])
-    target_cols = jnp.arange(patch_cols)
-    source_cols = jnp.arange(columns)
-    target_rows = jnp.arange(patch_rows)
-    source_rows = jnp.arange(strip_rows)
-
-    def place_group(total, item):
-        pixel_block_tile, block_offsets = item
-        column_selection = (
-            target_cols[None, None, :]
-            == block_offsets[:, 1][:, None, None] + source_cols[None, :, None]
-        ).astype(jnp.float32)
-        row_select = (
-            target_rows[None, :, None]
-            == block_offsets[:, 0][:, None, None] + source_rows[None, None, :]
-        ).astype(jnp.float32)
-        broadened_width = jnp.einsum(
-            "vmwn,vny->vmwy", pixel_block_tile, column_selection, precision=largest_value
-        )
-        return (
-            total
-            + jnp.einsum("gri,gkip->krp", row_select, broadened_width, precision=largest_value),
-            None,
-        )
-
-    start = jnp.zeros((2, patch_rows, patch_cols), jnp.float32)
-    placed, _ = lax.scan(place_group, start, (pairs, grouped_offsets))
-    return (placed[0], placed[1])
+def place_kernel(rows_ref, cols_ref, wts_ref, flux_ref, weight_ref, coadd_ref, wmap_ref, acc_n, acc_w):
+    slots, strip_rows, lanes = flux_ref.shape
+    lane_blocks = acc_n.shape[0] - 1
+    out_rows = coadd_ref.shape[0]
+    acc_n[...] = jnp.zeros(acc_n.shape, jnp.float32)
+    acc_w[...] = jnp.zeros(acc_w.shape, jnp.float32)
+    lane = lax.broadcasted_iota(jnp.int32, (strip_rows, lanes), 1)
+    sub = lax.broadcasted_iota(jnp.int32, (strip_rows, lanes), 0)
+
+    def body(s, carry):
+        r = rows_ref[s]
+        c = cols_ref[s]
+        wt = wts_ref[s]
+        q = c // lanes
+        rem = c - q * lanes
+        rq = r // strip_rows
+        rr = r - rq * strip_rows
+        lane_lo = lane >= rem
+        sub_lo = sub >= rr
+        top = pl.multiple_of(rq * strip_rows, strip_rows)
+        nxt = pl.multiple_of(top + strip_rows, strip_rows)
+        for src, acc in ((flux_ref, acc_n), (weight_ref, acc_w)):
+            v = src[s] * wt
+            v = pltpu.roll(v, rem, 1)
+            v = pltpu.roll(v, rr, 0)
+            zero = jnp.zeros_like(v)
+            a = jnp.where(sub_lo, v, zero)
+            b = v - a
+            acc[q, pl.ds(top, strip_rows), :] += jnp.where(lane_lo, a, zero)
+            acc[q + 1, pl.ds(top, strip_rows), :] += jnp.where(lane_lo, zero, a)
+            acc[q, pl.ds(nxt, strip_rows), :] += jnp.where(lane_lo, b, zero)
+            acc[q + 1, pl.ds(nxt, strip_rows), :] += jnp.where(lane_lo, zero, b)
+        return carry
+
+    lax.fori_loop(0, slots, body, 0)
+    for j in range(lane_blocks):
+        n = acc_n[j, pl.ds(0, out_rows), :]
+        w = acc_w[j, pl.ds(0, out_rows), :]
+        wmap_ref[:, pl.ds(j * lanes, lanes)] = w
+        coadd_ref[:, pl.ds(j * lanes, lanes)] = n / jnp.maximum(w, 1.0)
+
+
+def place(flux, weight, rows, cols, wts, patch_rows, patch_cols):
+    slots, strip_rows, lanes = flux.shape
+    lane_blocks = patch_cols // lanes
+    smem = pltpu.SMEM
+    return pl.pallas_call(
+        place_kernel,
+        out_shape=(
+            jax.ShapeDtypeStruct((patch_rows, patch_cols), jnp.float32),
+            jax.ShapeDtypeStruct((patch_rows, patch_cols), jnp.float32),
+        ),
+        in_specs=[
+            pl.BlockSpec(memory_space=smem),
+            pl.BlockSpec(memory_space=smem),
+            pl.BlockSpec(memory_space=smem),
+            pl.BlockSpec(memory_space=pltpu.VMEM),
+            pl.BlockSpec(memory_space=pltpu.VMEM),
+        ],
+        out_specs=(pl.BlockSpec(memory_space=pltpu.VMEM), pl.BlockSpec(memory_space=pltpu.VMEM)),
+        scratch_shapes=[
+            pltpu.VMEM((lane_blocks + 1, patch_rows + strip_rows, lanes), jnp.float32),
+            pltpu.VMEM((lane_blocks + 1, patch_rows + strip_rows, lanes), jnp.float32),
+        ],
+    )(rows, cols, wts, flux, weight)
 
 
 def shards(
@@ -180,11 +211,9 @@
     slot_weight = jnp.sum(slot_hot * visit_weight[None, :], axis=1)
     weight_body = got_first[:, :body_rows, :].reshape(slot_total, strip_rows, columns)
     flux_body = got_flux.reshape(slot_total, strip_rows, columns)
-    weight_body = weight_body * slot_weight[:, None, None]
-    flux_body = flux_body * slot_weight[:, None, None]
-    offsets = jnp.stack([slot_rows, slot_cols], axis=1)
-    numerator, weight_map = place_slots(flux_body, weight_body, offsets, PH, PW)
-    coadd_image = numerator / jnp.maximum(weight_map, 1.0)
+    coadd_image, weight_map = place(
+        flux_body, weight_body, slot_rows, slot_cols, slot_weight, PH, PW
+    )
     return (coadd_image[None], weight_map[None])
 
 

time: 82.4 us -> 74.9 us (0.909)
  matrix products: 22.9 us -> 5.49 us
  Pallas kernels: 0 us -> 11.9 us
  local copies, waits for them, and re-layouts: 9.19 us -> 11.7 us
  waiting for transfers between devices: 28.2 us -> 25.7 us
  other arithmetic: 9.37 us -> 7.62 us
    dot_general x16 -> x0, matrix products: 17.4 us -> none  [the longest x8 11.7 us: place_group(): jnp.einsum('vmwn,vny->vmwy', pixel_block_tile, column_selection, precisio...]
    pallas_call x0 -> x1, Pallas kernels: none -> 11.9 us  [place(): pl.pallas_call(place_kernel, out_shape=(jax.ShapeDtypeStruct((patch_rows,...]
    all_to_all x1, waiting for transfers between devices: 14.3 us -> 11.8 us  [shards(): lax.all_to_all(flux_packed, 'patch', split_axis=0, concat_axis=0, tiled=T...]
    convert_element_type x0 -> x2, local copies, waits for them, and re-layouts: none -> 1.27 us  [the longest x1 0.65 us: shards(): slot_cols = got_meta[:, 1, :capacity].reshape(slot_total).astype(jnp.int32)]
    add x16 -> x0, other arithmetic: 1.14 us -> none  [the longest x8 0.57 us: place_group(): block_offsets[:, 1][:, None, None] + source_cols[None, :, None]]
  transfers between devices with their start and end apart: 2 -> 2, of which waited for: 2 -> 2; matrix products, arithmetic and copies ran while one was open for 2% -> 6% of each run, Pallas kernels for 0% -> 0%
where the time goes in v3:
time: 74.9 us; the launch traced here: 74.3 us
  waiting for transfers between devices  25.7 us (34%)
  Pallas kernels  11.9 us (16%)
  local copies, waits for them, and re-layouts  11.7 us (16%)
  starting transfers between devices  10.9 us (15%)
  other arithmetic  7.62 us (10%)
  matrix products  5.49 us (7%)
  between operations  0.89 us (1%)
    all_to_all x1, waiting for transfers between devices, shards(): lax.all_to_all(first, 'patch', split_axis=0, concat_axis=0, tiled=True)  13.9 us
    pallas_call x1, Pallas kernels, place(): pl.pallas_call(place_kernel, out_shape=(jax.ShapeDtypeStruct((patch_rows,...  11.9 us
    all_to_all x1, waiting for transfers between devices, shards(): lax.all_to_all(flux_packed, 'patch', split_axis=0, concat_axis=0, tiled=T...  11.8 us
    all_to_all x1, starting transfers between devices, shards(): lax.all_to_all(first, 'patch', split_axis=0, concat_axis=0, tiled=True)  7.31 us
    reduce_sum x1, other arithmetic, convolve_all(): jnp.sum(col_ops[None, :, None, :, :, None, :] * fx[:, :, :, :, None, :, :...  4.17 us
    all_to_all x1, starting transfers between devices, shards(): lax.all_to_all(flux_packed, 'patch', split_axis=0, concat_axis=0, tiled=T...  3.64 us
    reduce_sum x1, local copies, waits for them, and re-layouts, convolve_all(): jnp.sum(col_ops[None, :, None, :, :, None, :] * fx[:, :, :, :, None, :, :...  3.31 us
    dot_general x1, matrix products, convolve_all(): fields = jnp.einsum('nqkiy,nkyz->nqiz', smooth, mixed, precision=mxu_value)  2.27 us
  transfers between devices with their start and end apart: 2, of which 2 were waited for; matrix products, arithmetic and copies ran while one was open for 6% of the time, Pallas kernels for 0%

profile of v3, /device:TPU:0, one launch (start us, length us, event | category | flops | bytes accessed | tf_op | source)
XLA Modules:
  0.0 74.3 jit_solution(10166355167532491336)
XLA Ops:
  0.7 0.8 %copy.58 = f32[2,27,6]{2,0,1:T(2,128)S(1)} copy(f32[2,27,6]{1,0,2:T(2,128)} %param.19) | data formatting | bytes 2592 | tf_op args[3]
  1.4 0.2 fusion.34
  1.7 0.2 copy.59
  1.9 0.2 copy.61
  2.1 0.2 copy.63
  2.3 0.2 copy.65
  2.6 0.2 copy.67
  2.8 0.2 copy.69
  3.0 0.4 multiply_add_fusion.1
  3.4 0.1 stack_broadcast_in_dim.2
  3.5 0.1 pad_maximum_fusion.1
  3.6 4.2 %multiply_reduce_fusion = f32[2,3,3,128,3,128]{5,3,4,2,1,0:T(8,128)} fusion(f32[2,3,3,3,3,128]{5,4,3,2,1,0:T(4,128)S(1)} %pad_maximum_fusion.1, f32[3,3,128,128]{3,2,1,0:T(8,128)} %constant.129.clone), kind=kLoop, calls=%fused_computation | loop fusion | flops 4423680 | bytes 4211712 | tf_op jit(solution)/shard_map/reduce_sum | solution.py:77
  7.8 3.3 %copy.71 = f32[2,3,3,128,3,128]{3,5,4,2,1,0:T(8,128)S(1)} copy(f32[2,3,3,128,3,128]{5,3,4,2,1,0:T(8,128)} %multiply_reduce_fusion) | data formatting | bytes 7077888 | tf_op jit(solution)/shard_map/reduce_sum | solution.py:77
  11.1 1.0 %pad_bitcast_fusion = f32[2,35,8,128]{3,2,1,0:T(8,128)S(1)} fusion(f32[2,256,128]{2,1,0:T(8,128)} %param.16), kind=kLoop, calls=%fused_computation.13 | loop fusion | bytes 548864 | tf_op jit(solution)/shard_map/reshape | solution.py:61
  12.0 0.1 fusion.33
  12.1 1.8 %fusion.5 = f32[2,32,128,9,8]{2,4,3,1,0:T(8,128)S(1)} fusion(f32[9,8,32,1,1]{2,1,0,4,3:T(8,128)} %constant.139, f32[2,32,8,128]{3,2,1,0:T(8,128)S(1)} %get-tuple-element.54, f32[2,32,8,128]{3,2,1,0:T(8,128)S(1)} %get-tuple-element.55, f32[2,32,8,128]{3,2,1,0:T(8,128)S(1)} %get-tuple-element.56, f32[2,32,8,128]{3,2,1,0:T(8,128)S(1)} %get-tuple-element.53), kind=kOutput, calls=%fused_computation.5 | convolution fusion | flops 114032640 | bytes 3417088 | tf_op jit(solution)/shard_map/kit,nqtx->nqkix/dot_general | solution.py:64
  14.0 0.0 copy-start.1
  14.0 0.0 copy-start.3
  14.0 0.0 copy-start.2
  14.0 2.3 %fusion.2 = f32[2,256,384]{2,1,0:T(8,128)S(1)} fusion(f32[2,9,128,384,1]{2,3,1,4,0:T(8,128)S(1)} %bitcast.50, f32[2,32,128,9,8]{2,4,3,1,0:T(8,128)S(1)} %fusion.5), kind=kOutput, calls=%fused_computation.3 | convolution fusion | flops 1358954496 | bytes 6684672 | tf_op jit(solution)/shard_map/nqkiy,nkyz->nqiz/dot_general | solution.py:81
  16.3 0.0 copy-done.1
  16.3 0.1 fusion.13
  16.4 0.1 reshape.204
  16.5 1.1 %select_reduce_fusion = (f32[2]{0:T(128)S(1)}, f32[2]{0:T(128)S(1)}) fusion(pred[2,256,128]{2,1,0:T(32,128)(4,1)S(1)} %get-tuple-element.52, f32[2,256,128]{2,1,0:T(8,128)} %param.17), kind=kLoop, calls=%fused_computation.19 | loop fusion | flops 262140 | bytes 327696 | tf_op jit(solution)/shard_map/reduce_sum | solution.py:170
  17.6 0.0 copy-done.3
  17.6 0.2 convert_reduce_fusion.1
  17.8 0.0 copy-done.2
  17.8 0.1 broadcast_in_dim.6
  17.9 0.1 stack_reshape.3
  18.0 0.8 %fusion.16 = f32[128,3]{0,1:T(4,128)S(1)} fusion(s32[64]{0:T(128)S(1)} %multiply_add_fusion.4, s32[64,1]{0,1:T(1,128)S(1)} %stack_reshape.3, s32[64,1]{0,1:T(1,128)} %bitcast.66, s32[64,1]{0,1:T(1,128)} %bitcast.67), kind=kOutput, calls=%fused_computation.25 | convolution fusion | flops 303680 | bytes 2560 | tf_op jit(solution)/shard_map/dot_general | solution.py:183
  18.8 0.1 reshape.206
  18.9 0.2 fusion.17
  19.2 0.1 reshape.205
  19.3 0.1 select_reduce_fusion.2
  19.4 0.3 scatter.11
  19.7 0.3 scatter.14
  19.9 0.8 %pad_maximum_fusion = f32[8,136,128]{2,1,0:T(8,128)} fusion(f32[8,8,128]{2,1,0:T(8,128)S(1)} %scatter.14, f32[8,128,128]{2,1,0:T(8,128)S(1)} %reshape.205), kind=kLoop, calls=%fused_computation.12 | loop fusion | flops 139264 | bytes 1114112 | tf_op jit(solution)/shard_map/concatenate | solution.py:193
  20.8 7.3 %all-to-all-start = ((f32[8,136,128]{2,1,0:T(8,128)}), f32[8,136,128]{2,1,0:T(8,128)S(1)}, u32[]{:S(2)}, u32[]{:S(2)}) async-start(f32[8,136,128]{2,1,0:T(8,128)} %pad_maximum_fusion), calls=%async_computation | async-start | bytes 1114112 | tf_op jit(solution)/shard_map/all_to_all | solution.py:194
  28.1 0.4 fusion.15
  28.5 0.9 %reshape.212 = f32[8,128,128]{2,1,0:T(8,128)} reshape(f32[128,1024]{1,0:T(8,128)S(1)} %fusion.15) | data formatting | bytes 1048576 | tf_op jit(solution)/shard_map/reshape | solution.py:198
  29.4 13.9 %all-to-all-done = f32[8,136,128]{2,1,0:T(8,128)S(1)} async-done(((f32[8,136,128]{2,1,0:T(8,128)}), f32[8,136,128]{2,1,0:T(8,128)S(1)}, u32[]{:S(2)}, u32[]{:S(2)}) %all-to-all-start) | async-done | bytes 557088 | tf_op jit(solution)/shard_map/all_to_all | solution.py:194
  43.3 3.6 %all-to-all-start.1 = ((f32[8,128,128]{2,1,0:T(8,128)}), f32[8,128,128]{2,1,0:T(8,128)S(1)}, u32[]{:S(2)}, u32[]{:S(2)}) async-start(f32[8,128,128]{2,1,0:T(8,128)} %reshape.212), calls=%async_computation.1 | async-start | bytes 1048576 | tf_op jit(solution)/shard_map/all_to_all | solution.py:201
  46.9 0.1 convert_element_type.68
  47.0 0.6 convert_element_type.64.rows_ref
  47.6 0.7 convert_element_type.66.cols_ref
  48.3 0.8 %slice.180 = f32[8,128,128]{2,1,0:T(8,128)} slice(f32[8,136,128]{2,1,0:T(8,128)S(1)} %all-to-all-done), slice={[0:8], [0:128], [0:128]} | slice | bytes 1048576 | tf_op jit(solution)/shard_map/slice | solution.py:212
  49.2 0.6 select_reduce_fusion.1.wts_ref
  49.7 11.8 %all-to-all-done.1 = f32[8,128,128]{2,1,0:T(8,128)S(1)} async-done(((f32[8,128,128]{2,1,0:T(8,128)}), f32[8,128,128]{2,1,0:T(8,128)S(1)}, u32[]{:S(2)}, u32[]{:S(2)}) %all-to-all-start.1) | async-done | bytes 524320 | tf_op jit(solution)/shard_map/all_to_all | solution.py:201
  61.6 0.0 copy-start
  61.6 0.8 %copy-done = f32[8,128,128]{2,1,0:T(8,128)} copy-done((f32[8,128,128]{2,1,0:T(8,128)}, f32[8,128,128]{2,1,0:T(8,128)S(1)}, u32[]{:S(2)}) %copy-start) | copy-done | bytes 524312
  62.4 11.9 %shard_map.113 = (f32[128,512]{1,0:T(8,128)}, f32[128,512]{1,0:T(8,128)}) custom-call(s32[128]{0:T(128)} %convert_element_type.64.rows_ref, s32[128]{0:T(128)} %convert_element_type.66.cols_ref, f32[128]{0:T(128)} %select_reduce_fusion.1.wts_ref, f32[128,8,128]{2,1,0:T(8,128)} %bitcast.51, f32[128,8,128]{2,1,0:T(8,128)} %bitcast.52), custom_call_target="tpu_custom_call" | custom-call | tf_op jit(solution)/shard_map/pallas_call | solution.py:137
  (17 shorter events, 0.2 us)
Async XLA Ops:
  14.0 2.3 %copy-start.1 = (s32[2,256,128]{2,1,0:T(8,128)S(1)}, s32[2,256,128]{2,1,0:T(8,128)}, u32[]{:S(2)}) copy-start(s32[2,256,128]{2,1,0:T(8,128)} %param.18) | copy-start | bytes 786436
  14.0 3.7 %copy-start.3 = (s32[64,1]{0,1:T(1,128)S(1)}, s32[64,1]{0,1:T(1,128)}, u32[]{:S(2)}) copy-start(s32[64,1]{0,1:T(1,128)} %param.21) | copy-start | bytes 772
  14.0 3.8 %copy-start.2 = (s32[2,1]{0,1:T(1,128)S(1)}, s32[2,1]{0,1:T(1,128)}, u32[]{:S(2)}) copy-start(s32[2,1]{0,1:T(1,128)} %param.20) | copy-start | bytes 28
  20.8 22.5 %all-to-all-start = ((f32[8,136,128]{2,1,0:T(8,128)}), f32[8,136,128]{2,1,0:T(8,128)S(1)}, u32[]{:S(2)}, u32[]{:S(2)}) async-start(f32[8,136,128]{2,1,0:T(8,128)} %pad_maximum_fusion), calls=%async_computation | async-start | bytes 1114112 | tf_op jit(solution)/shard_map/all_to_all | solution.py:194
  43.3 18.3 %all-to-all-start.1 = ((f32[8,128,128]{2,1,0:T(8,128)}), f32[8,128,128]{2,1,0:T(8,128)S(1)}, u32[]{:S(2)}, u32[]{:S(2)}) async-start(f32[8,128,128]{2,1,0:T(8,128)} %reshape.212), calls=%async_computation.1 | async-start | bytes 1048576 | tf_op jit(solution)/shard_map/all_to_all | solution.py:201
  61.6 0.8 %copy-start = (f32[8,128,128]{2,1,0:T(8,128)}, f32[8,128,128]{2,1,0:T(8,128)S(1)}, u32[]{:S(2)}) copy-start(f32[8,128,128]{2,1,0:T(8,128)S(1)} %all-to-all-done.1) | copy-start | bytes 1572868

commit v4 on v3

--- a/solution.py
+++ b/solution.py
@@ -88,8 +88,9 @@
     )
 
 
-def place_kernel(rows_ref, cols_ref, wts_ref, flux_ref, weight_ref, coadd_ref, wmap_ref, acc_n, acc_w):
-    slots, strip_rows, lanes = flux_ref.shape
+def place_kernel(rows_ref, cols_ref, wts_ref, tiles_ref, coadd_ref, wmap_ref, acc_n, acc_w):
+    slots, tile_rows, lanes = tiles_ref.shape
+    strip_rows = tile_rows // 2
     lane_blocks = acc_n.shape[0] - 1
     out_rows = coadd_ref.shape[0]
     acc_n[...] = jnp.zeros(acc_n.shape, jnp.float32)
@@ -109,8 +110,8 @@
         sub_lo = sub >= rr
         top = pl.multiple_of(rq * strip_rows, strip_rows)
         nxt = pl.multiple_of(top + strip_rows, strip_rows)
-        for src, acc in ((flux_ref, acc_n), (weight_ref, acc_w)):
-            v = src[s] * wt
+        for part, acc in ((1, acc_n), (0, acc_w)):
+            v = tiles_ref[s, pl.ds(part * strip_rows, strip_rows), :] * wt
             v = pltpu.roll(v, rem, 1)
             v = pltpu.roll(v, rr, 0)
             zero = jnp.zeros_like(v)
@@ -122,7 +123,7 @@
             acc[q + 1, pl.ds(nxt, strip_rows), :] += jnp.where(lane_lo, zero, b)
         return carry
 
-    lax.fori_loop(0, slots, body, 0)
+    lax.fori_loop(0, slots, body, 0, unroll=4)
     for j in range(lane_blocks):
         n = acc_n[j, pl.ds(0, out_rows), :]
         w = acc_w[j, pl.ds(0, out_rows), :]
@@ -130,8 +131,9 @@
         coadd_ref[:, pl.ds(j * lanes, lanes)] = n / jnp.maximum(w, 1.0)
 
 
-def place(flux, weight, rows, cols, wts, patch_rows, patch_cols):
-    slots, strip_rows, lanes = flux.shape
+def place(tiles, rows, cols, wts, patch_rows, patch_cols):
+    slots, tile_rows, lanes = tiles.shape
+    strip_rows = tile_rows // 2
     lane_blocks = patch_cols // lanes
     smem = pltpu.SMEM
     return pl.pallas_call(
@@ -145,14 +147,13 @@
             pl.BlockSpec(memory_space=smem),
             pl.BlockSpec(memory_space=smem),
             pl.BlockSpec(memory_space=pltpu.VMEM),
-            pl.BlockSpec(memory_space=pltpu.VMEM),
         ],
         out_specs=(pl.BlockSpec(memory_space=pltpu.VMEM), pl.BlockSpec(memory_space=pltpu.VMEM)),
         scratch_shapes=[
             pltpu.VMEM((lane_blocks + 1, patch_rows + strip_rows, lanes), jnp.float32),
             pltpu.VMEM((lane_blocks + 1, patch_rows + strip_rows, lanes), jnp.float32),
         ],
-    )(rows, cols, wts, flux, weight)
+    )(rows, cols, wts, tiles)
 
 
 def shards(
@@ -186,21 +187,20 @@
     meta = meta.at[:, 3, :VISITS].set(jnp.broadcast_to(local_count, (devices, VISITS)))
     meta = meta.at[:, 4, :VISITS].set(jnp.broadcast_to(local_load, (devices, VISITS)))
     body_rows = capacity * strip_rows
-    weight_tiles = usable.reshape(strip_total, strip_rows * columns)
-    weight_packed = jnp.dot(chooser, weight_tiles, precision=largest_value).reshape(
-        devices, body_rows, columns
-    )
-    first = jnp.concatenate([weight_packed, meta], axis=1)
-    got_first = lax.all_to_all(first, "patch", split_axis=0, concat_axis=0, tiled=True)
-
     convolved = convolve_all(exposures, kernel_coeffs)
-    flux_tiles = (usable * convolved).reshape(strip_total, strip_rows * columns)
-    flux_packed = jnp.dot(chooser, flux_tiles, precision=largest_value).reshape(
-        devices, body_rows, columns
-    )
-    got_flux = lax.all_to_all(flux_packed, "patch", split_axis=0, concat_axis=0, tiled=True)
-
-    got_meta = got_first[:, body_rows:, :]
+    tiles = jnp.concatenate(
+        [
+            usable.reshape(strip_total, strip_rows * columns),
+            (usable * convolved).reshape(strip_total, strip_rows * columns),
+        ],
+        axis=1,
+    )
+    packed = jnp.dot(chooser, tiles, precision=largest_value).reshape(
+        devices, 2 * body_rows, columns
+    )
+    payload = jnp.concatenate([packed, meta], axis=1)
+    got = lax.all_to_all(payload, "patch", split_axis=0, concat_axis=0, tiled=True)
+    got_meta = got[:, 2 * body_rows :, :]
     visit_count = jnp.sum(got_meta[:, 3, :VISITS], axis=0)
     visit_load = jnp.sum(got_meta[:, 4, :VISITS], axis=0)
     visit_weight = (visit_count + 1.0) / (visit_load + 1.0)
@@ -209,11 +209,8 @@
     slot_visit = got_meta[:, 2, :capacity].reshape(slot_total).astype(jnp.int32)
     slot_hot = (slot_visit[:, None] == jnp.arange(VISITS)[None, :]).astype(jnp.float32)
     slot_weight = jnp.sum(slot_hot * visit_weight[None, :], axis=1)
-    weight_body = got_first[:, :body_rows, :].reshape(slot_total, strip_rows, columns)
-    flux_body = got_flux.reshape(slot_total, strip_rows, columns)
-    coadd_image, weight_map = place(
-        flux_body, weight_body, slot_rows, slot_cols, slot_weight, PH, PW
-    )
+    body = got[:, : 2 * body_rows].reshape(slot_total, 2 * strip_rows, columns)
+    coadd_image, weight_map = place(body, slot_rows, slot_cols, slot_weight, PH, PW)
     return (coadd_image[None], weight_map[None])
 
 

time: 74.9 us -> 68.7 us (0.917)
  blocking collectives: 0 us -> 34.3 us
  waiting for transfers between devices: 25.7 us -> 0 us
  starting transfers between devices: 10.9 us -> 0 us
  Pallas kernels: 11.9 us -> 5.28 us
  local copies, waits for them, and re-layouts: 11.7 us -> 14.8 us
    all_to_all x0 -> x1, blocking collectives: none -> 34.3 us  [shards(): lax.all_to_all(payload, 'patch', split_axis=0, concat_axis=0, tiled=True)]
    all_to_all x2 -> x0, waiting for transfers between devices: 25.7 us -> none  [the longest x1 13.9 us: shards(): lax.all_to_all(first, 'patch', split_axis=0, concat_axis=0, tiled=True)]
    all_to_all x2 -> x0, starting transfers between devices: 10.9 us -> none  [the longest x1 7.31 us: shards(): lax.all_to_all(first, 'patch', split_axis=0, concat_axis=0, tiled=True)]
    pallas_call x1, Pallas kernels: 11.9 us -> 5.28 us  [place(): pl.pallas_call(place_kernel, out_shape=(jax.ShapeDtypeStruct((patch_rows,...]
    reshape x2, local copies, waits for them, and re-layouts: 0.11 us -> 1.45 us  [shards(): jnp.dot(chooser, placement, precision=largest_value)]
    slice x1, local copies, waits for them, and re-layouts: 0.07 us -> 1.03 us  [convolve_all(): padded[:, j:j + blocks]]
    reduce_sum x1, other arithmetic: 1.12 us -> 0.21 us  [shards(): jnp.sum(usable * variance, axis=(1, 2))[:, None] * visit_hot]
    convert_element_type x0 -> x1, other arithmetic: none -> 0.76 us  [shards(): usable = (jnp.bitwise_and(mask_bits, 3) != 3).astype(jnp.float32)]
  transfers between devices with their start and end apart: 2 -> 0, of which waited for: 2 -> 0; matrix products, arithmetic and copies ran while one was open for 6% -> 0% of each run, Pallas kernels for 0% -> 0%
where the time goes in v4:
time: 68.7 us; the launch traced here: 68.3 us
  blocking collectives  34.3 us (50%)
  local copies, waits for them, and re-layouts  14.8 us (22%)
  other arithmetic  7.15 us (10%)
  matrix products  5.83 us (8%)
  Pallas kernels  5.28 us (8%)
  between operations  0.94 us (1%)
    all_to_all x1, blocking collectives, shards(): lax.all_to_all(payload, 'patch', split_axis=0, concat_axis=0, tiled=True)  34.3 us
    pallas_call x1, Pallas kernels, place(): pl.pallas_call(place_kernel, out_shape=(jax.ShapeDtypeStruct((patch_rows,...  5.28 us
    reduce_sum x1, other arithmetic, convolve_all(): jnp.sum(col_ops[None, :, None, :, :, None, :] * fx[:, :, :, :, None, :, :...  4.17 us
    reduce_sum x1, local copies, waits for them, and re-layouts, convolve_all(): jnp.sum(col_ops[None, :, None, :, :, None, :] * fx[:, :, :, :, None, :, :...  3.31 us
    dot_general x1, matrix products, convolve_all(): fields = jnp.einsum('nqkiy,nkyz->nqiz', smooth, mixed, precision=mxu_value)  2.27 us
    dot_general x1, matrix products, convolve_all(): smooth = jnp.einsum('kit,nqtx->nqkix', rows, windows, precision=mxu_value)  2.25 us
    slice x8, local copies, waits for them, and re-layouts, convolve_all(): c = [coef[..., p, None] for p in range(6)]  1.54 us
    reshape x2, local copies, waits for them, and re-layouts, shards(): jnp.dot(chooser, placement, precision=largest_value)  1.45 us

profile of v4, /device:TPU:0, one launch (start us, length us, event | category | flops | bytes accessed | tf_op | source)
XLA Modules:
  0.0 68.3 jit_solution(12646034489277485348)
XLA Ops:
  0.6 0.5 multiply_add_fusion.2
  1.2 0.8 %copy.57 = f32[2,27,6]{2,0,1:T(2,128)S(1)} copy(f32[2,27,6]{1,0,2:T(2,128)} %param.19) | data formatting | bytes 2592 | tf_op args[3]
  2.0 0.2 fusion.37
  2.2 0.2 copy.58
  2.4 0.2 copy.60
  2.6 0.2 copy.62
  2.9 0.2 copy.64
  3.1 0.2 copy.66
  3.3 0.2 copy.68
  3.5 0.4 multiply_add_fusion.1
  3.9 0.1 stack_broadcast_in_dim.2
  4.0 0.1 pad_maximum_fusion.1
  4.1 4.2 %multiply_reduce_fusion = f32[2,3,3,128,3,128]{5,3,4,2,1,0:T(8,128)} fusion(f32[2,3,3,3,3,128]{5,4,3,2,1,0:T(4,128)S(1)} %pad_maximum_fusion.1, f32[3,3,128,128]{3,2,1,0:T(8,128)} %constant.129.clone), kind=kLoop, calls=%fused_computation | loop fusion | flops 4423680 | bytes 4211712 | tf_op jit(solution)/shard_map/reduce_sum | solution.py:77
  8.3 3.3 %copy.70 = f32[2,3,3,128,3,128]{3,5,4,2,1,0:T(8,128)S(1)} copy(f32[2,3,3,128,3,128]{5,3,4,2,1,0:T(8,128)} %multiply_reduce_fusion) | data formatting | bytes 7077888 | tf_op jit(solution)/shard_map/reduce_sum | solution.py:77
  11.6 0.0 copy-start.1
  11.6 0.0 copy-start.7
  11.6 0.0 copy-start.9
  11.6 0.0 copy-start.10
  11.6 0.0 copy-start.11
  11.6 1.1 %pad_bitcast_fusion = f32[2,35,8,128]{3,2,1,0:T(8,128)S(1)} fusion(f32[2,256,128]{2,1,0:T(8,128)} %param.16), kind=kLoop, calls=%fused_computation.17 | loop fusion | bytes 548864 | tf_op jit(solution)/shard_map/reshape | solution.py:61
  12.7 1.0 %fusion.36 = (f32[2,32,8,128]{3,2,1,0:T(8,128)}, f32[2,32,8,128]{3,2,1,0:T(8,128)}, f32[2,32,8,128]{3,2,1,0:T(8,128)}, f32[2,32,8,128]{3,2,1,0:T(8,128)}) fusion(f32[2,35,8,128]{3,2,1,0:T(8,128)S(1)} %pad_bitcast_fusion), kind=kLoop, calls=%fused_computation.65 | loop fusion | bytes 2097152 | tf_op jit(solution)/shard_map/slice | solution.py:62
  13.7 0.0 copy-done.1
  13.7 0.8 %fusion.35 = (f32[2,256,128]{2,1,0:T(8,128)}, pred[2,256,128]{2,1,0:T(8,128)(4,1)}) fusion(s32[2,256,128]{2,1,0:T(8,128)S(1)} %copy-done.1), kind=kLoop, calls=%fused_computation.64 | loop fusion | flops 196608 | bytes 589824 | tf_op jit(solution)/shard_map/convert_element_type | solution.py:168
  14.5 0.0 copy-done.7
  14.5 0.1 broadcast_in_dim.6
  14.6 0.6 stack_reshape.3
  15.2 0.0 copy-done.9
  15.2 0.2 convert_reduce_fusion.1
  15.4 0.0 copy-start.5
  15.4 0.6 copy-done.5
  15.9 0.0 copy-done.10
  15.9 0.0 copy-done.11
  15.9 0.7 %fusion.19 = f32[128,3]{0,1:T(4,128)S(1)} fusion(s32[64]{0:T(128)S(1)} %multiply_add_fusion.4, s32[64,1]{0,1:T(1,128)} %stack_reshape.3, s32[64,1]{0,1:T(1,128)S(1)} %bitcast.62, s32[64,1]{0,1:T(1,128)S(1)} %bitcast.63), kind=kOutput, calls=%fused_computation.28 | convolution fusion | flops 303680 | bytes 2560 | tf_op jit(solution)/shard_map/dot_general | solution.py:184
  16.7 0.7 %reshape.205 = f32[8,16,3]{1,0,2:T(8,128)} reshape(f32[128,3]{0,1:T(4,128)S(1)} %fusion.19) | data formatting | bytes 3072 | tf_op jit(solution)/shard_map/reshape | solution.py:184
  17.4 0.7 %copy.80 = f32[8,16,3]{1,2,0:T(4,128)S(1)} copy(f32[8,16,3]{1,0,2:T(8,128)} %reshape.205) | data formatting | bytes 3072 | tf_op jit(solution)/shard_map/reshape | solution.py:184
  18.1 2.3 %fusion.5 = f32[2,32,128,9,8]{2,4,3,1,0:T(8,128)S(1)} fusion(f32[9,8,32,1,1]{2,1,0,4,3:T(8,128)} %constant.139, f32[2,32,8,128]{3,2,1,0:T(8,128)} %get-tuple-element.54, f32[2,32,8,128]{3,2,1,0:T(8,128)} %get-tuple-element.55, f32[2,32,8,128]{3,2,1,0:T(8,128)} %get-tuple-element.56, f32[2,32,8,128]{3,2,1,0:T(8,128)} %get-tuple-element.53), kind=kOutput, calls=%fused_computation.6 | convolution fusion | flops 114032640 | bytes 3417088 | tf_op jit(solution)/shard_map/kit,nqtx->nqkix/dot_general | solution.py:64
  20.4 0.0 copy-start
  20.4 0.0 copy-start.2
  20.4 0.0 copy-start.3
  20.4 0.0 copy-start.4
  20.4 2.3 %fusion.2 = f32[2,256,384]{2,1,0:T(8,128)S(1)} fusion(f32[2,9,128,384,1]{2,3,1,4,0:T(8,128)S(1)} %bitcast.47, f32[2,32,128,9,8]{2,4,3,1,0:T(8,128)S(1)} %fusion.5), kind=kOutput, calls=%fused_computation.3 | convolution fusion | flops 1358954496 | bytes 6684672 | tf_op jit(solution)/shard_map/nqkiy,nkyz->nqiz/dot_general | solution.py:81
  22.7 0.0 copy-start.6
  22.7 0.0 copy-done
  22.7 0.0 copy-done.2
  22.7 0.0 copy-done.3
  22.8 0.0 copy-done.4
  22.8 0.2 select_reduce_fusion
  23.0 0.0 copy-start.8
  23.1 1.0 %reshape.198 = f32[64,1024]{1,0:T(8,128)S(1)} reshape(f32[2,256,128]{2,1,0:T(8,128)} %get-tuple-element.51) | data formatting | bytes 524288 | tf_op jit(solution)/shard_map/reshape | solution.py:193
  24.1 0.0 copy-done.6
  24.1 0.6 fusion.12
  24.6 0.2 reshape.204
  24.8 0.0 copy-done.8
  24.8 0.1 select_reduce_fusion.2
  24.9 0.3 scatter.11
  25.2 0.3 scatter.14
  25.5 0.1 pad_maximum_fusion
  25.6 34.3 %all_to_all.5 = f32[8,264,128]{2,1,0:T(8,128)S(1)} all-to-all(f32[8,264,128]{2,1,0:T(8,128)S(1)} %pad_maximum_fusion), channel_id=1, replica_groups=mesh['patch'=8,'band'=4] {'patch'}, dimensions={0} | all-to-all | bytes 2162688 | tf_op jit(solution)/shard_map/all_to_all | solution.py:202
  59.9 0.1 convert_element_type.70
  60.0 0.7 convert_element_type.66.rows_ref
  60.7 0.6 convert_element_type.68.cols_ref
  61.3 0.6 select_reduce_fusion.1.wts_ref
  61.9 1.1 %slice.180 = f32[8,256,128]{2,1,0:T(8,128)} slice(f32[8,264,128]{2,1,0:T(8,128)S(1)} %all_to_all.5), slice={[0:8], [0:256], [0:128]} | slice | bytes 2097152 | tf_op jit(solution)/shard_map/slice | solution.py:212
  63.0 5.3 %shard_map.113 = (f32[128,512]{1,0:T(8,128)}, f32[128,512]{1,0:T(8,128)}) custom-call(s32[128]{0:T(128)} %convert_element_type.66.rows_ref, s32[128]{0:T(128)} %convert_element_type.68.cols_ref, f32[128]{0:T(128)} %select_reduce_fusion.1.wts_ref, f32[128,16,128]{2,1,0:T(8,128)} %bitcast.48), custom_call_target="tpu_custom_call" | custom-call | tf_op jit(solution)/shard_map/pallas_call | solution.py:139
  (15 shorter events, 0.2 us)
Async XLA Ops:
  11.6 2.1 %copy-start.1 = (s32[2,256,128]{2,1,0:T(8,128)S(1)}, s32[2,256,128]{2,1,0:T(8,128)}, u32[]{:S(2)}) copy-start(s32[2,256,128]{2,1,0:T(8,128)} %param.18) | copy-start | bytes 786436
  11.6 2.9 %copy-start.7 = (s32[2,1]{0,1:T(1,128)S(1)}, s32[2,1]{0,1:T(1,128)}, u32[]{:S(2)}) copy-start(s32[2,1]{0,1:T(1,128)} %param.20) | copy-start | bytes 28
  11.6 3.6 %copy-start.9 = (s32[64,1]{0,1:T(1,128)S(1)}, s32[64,1]{0,1:T(1,128)}, u32[]{:S(2)}) copy-start(s32[64,1]{0,1:T(1,128)} %param.21) | copy-start | bytes 772
  11.6 4.3 %copy-start.10 = (s32[64]{0:T(128)S(1)}, s32[64]{0:T(128)}, u32[]{:S(2)}) copy-start(s32[64]{0:T(128)} %param.23) | copy-start | bytes 772
  11.6 4.3 %copy-start.11 = (s32[64]{0:T(128)S(1)}, s32[64]{0:T(128)}, u32[]{:S(2)}) copy-start(s32[64]{0:T(128)} %param.22) | copy-start | bytes 772
  15.4 0.6 copy-start.5
  20.4 2.3 %copy-start = (pred[2,256,128]{2,1,0:T(8,128)(4,1)S(1)}, pred[2,256,128]{2,1,0:T(8,128)(4,1)}, u32[]{:S(2)}) copy-start(pred[2,256,128]{2,1,0:T(8,128)(4,1)} %get-tuple-element.52) | copy-start | bytes 196612
  20.4 2.3 %copy-start.2 = (f32[2,256,128]{2,1,0:T(8,128)S(1)}, f32[2,256,128]{2,1,0:T(8,128)}, u32[]{:S(2)}) copy-start(f32[2,256,128]{2,1,0:T(8,128)} %param.17) | copy-start | bytes 786436
  20.4 2.3 %copy-start.3 = (f32[256]{0:T(256)S(1)}, f32[256]{0:T(256)}, u32[]{:S(2)}) copy-start(f32[256]{0:T(256)} %get-tuple-element.68) | copy-start | bytes 3076
  20.4 2.3 %copy-start.4 = (f32[256]{0:T(256)S(1)}, f32[256]{0:T(256)}, u32[]{:S(2)}) copy-start(f32[256]{0:T(256)} %get-tuple-element.69) | copy-start | bytes 3076
  22.7 1.3 %copy-start.6 = (s32[64]{0:T(128)S(1)}, s32[64]{0:T(128)}, u32[]{:S(2)}) copy-start(s32[64]{0:T(128)} %copy-done.5) | copy-start | bytes 772
  23.0 1.8 %copy-start.8 = (s32[2,1]{0,1:T(1,128)S(1)}, s32[2,1]{0,1:T(1,128)}, u32[]{:S(2)}) copy-start(s32[2,1]{0,1:T(1,128)} %param.20) | copy-start | bytes 28
